TPU v7x, 32 devices: a whole 2x2x4 slice. The times are simulated.
32 devices in a mesh: groups: 1, orb: 32 (over z, y, x, core), aux: 1.
Axes of the slice: x: 2, y: 2, z: 4, core: 2. Of those that a mesh axis runs over, the one named last changes fastest.
Arguments:
- exchange_integral_halves: float32 [1, 128, 256, 256], P('aux', ('groups', 'orb')), may hold values from -3 to 3
- amplitudes: bfloat16 [128, 256, 256], P(('groups', 'orb')), may hold values from -6 to 6
- pair_slot_orbitals: int32 [128, 2], P('groups'), may hold values from 0 to 63
- pao_domain: int32 [64, 256], P('groups'), may hold values from 0 to 511, as said below
- pao_intersection: bfloat16 [512, 512], P('groups'), as said below
- pao_fock: bfloat16 [512, 512], P('groups'), as said below
- occ_energy: float32 [64], P('groups'), may hold values from -1.5 to -0.3
- coupled_pair_owner: int32 [128, 8], P(('groups', 'orb')), may hold values from 0 to 31, all different within a row; in each aligned block of 4 rows (0 to 3, 4 to 7, ...) at most 2 rows name the same one
- coupled_pair_slot: int32 [128, 8], P(('groups', 'orb')), may hold values from 0 to 3
- coupling_swap_flag: int32 [128, 8], P(('groups', 'orb')), may hold values from 0 to 1
- coupling_fock_element: float32 [128, 8], P(('groups', 'orb')), may hold values from -1.2 to 1.2
Outputs:
- residual: float32 [128, 256, 256], P(('groups', 'orb'), 'aux')
- updated_pair_amplitudes: bfloat16 [128, 256, 256], P(('groups', 'orb'), 'aux')
Inputs may be any that keep to these rules, and one draw needn't show every extreme that they name: `pao_domain`: each orbital's 256 domain entries are distinct. `coupled_pair_owner`: the 8 owners in one row differ; among the 4 pair slots of one owner no owner is named by more than 2 rows, a bound that some block reaches. `pao_intersection`: symmetric with unit diagonal. `pao_fock`: symmetric with diagonal from 0.5 to 3.
All inputs are finite; a program needn't handle non-finite values.
Results may differ from a plain program's by a relative error of at most 0.012.
Values may be sent and summed in bfloat16 or wider, within the bound.
No kernel may reach another device: no remote copies, remote signals or barrier semaphores. Data moves between devices by JAX's collectives and lax.ppermute only.
A program may use at most 128 MiB of HBM per device.

v0:
```python
import jax
import jax.numpy as jnp
from jax import lax
from jax.sharding import PartitionSpec as P


def one_hot(ids, width):
    return (ids[..., None] == jnp.arange(width, dtype=ids.dtype)).astype(jnp.bfloat16)


def sel_rows(onehot, matrix):
    return jnp.einsum(
        "...rk,kc->...rc", onehot, matrix, preferred_element_type=jnp.float32
    ).astype(jnp.bfloat16)


def shards(
    exchange_integral_halves,
    amplitudes,
    pair_slot_orbitals,
    pao_domain,
    pao_intersection,
    pao_fock,
    occ_energy,
    coupled_pair_owner,
    coupled_pair_slot,
    coupling_swap_flag,
    coupling_fock_element,
):
    slot_count, extent = amplitudes.shape[0], amplitudes.shape[1]
    paos = pao_intersection.shape[0]
    halves = lax.axis_size("aux")
    owner_index = lax.axis_index("orb")
    aux_index = lax.axis_index("aux")
    half_rows = extent // halves
    row_first = aux_index * half_rows

    every_amp = lax.all_gather(amplitudes, "orb", axis=0, tiled=True)

    own_slots = owner_index * slot_count + jnp.arange(slot_count, dtype=jnp.int32)
    orb_i = pair_slot_orbitals[own_slots, 0]
    orb_j = pair_slot_orbitals[own_slots, 1]
    dom_i = pao_domain[orb_i]
    dom_j = pao_domain[orb_j]
    rows_dom = lax.dynamic_slice_in_dim(dom_i, row_first, half_rows, 1)
    energy_sum = occ_energy[orb_i] + occ_energy[orb_j]

    global_slot = coupled_pair_owner * slot_count + coupled_pair_slot
    flipped = coupling_swap_flag == 1
    first_orb = pair_slot_orbitals[global_slot, 0]
    second_orb = pair_slot_orbitals[global_slot, 1]
    orb_p = jnp.where(flipped, second_orb, first_orb)
    orb_q = jnp.where(flipped, first_orb, second_orb)

    oh_rows = one_hot(rows_dom, paos)
    oh_i = one_hot(dom_i, paos)
    oh_j = one_hot(dom_j, paos)
    oh_p = one_hot(pao_domain[orb_p], paos)
    oh_q = one_hot(pao_domain[orb_q], paos)

    rs = sel_rows(oh_rows, pao_intersection)
    rf = sel_rows(oh_rows, pao_fock)
    s_ii = jnp.einsum("brk,bak->bra", rs, oh_i, preferred_element_type=jnp.float32).astype(jnp.bfloat16)
    f_ii = jnp.einsum("brk,bak->bra", rf, oh_i, preferred_element_type=jnp.float32).astype(jnp.bfloat16)
    js = sel_rows(oh_j, pao_intersection)
    jf = sel_rows(oh_j, pao_fock)
    s_jj = jnp.einsum("bjk,bak->bja", js, oh_j, preferred_element_type=jnp.float32).astype(jnp.bfloat16)
    f_jj = jnp.einsum("bjk,bak->bja", jf, oh_j, preferred_element_type=jnp.float32).astype(jnp.bfloat16)
    col_s = jnp.einsum("kc,bjc->bkj", pao_intersection, oh_j, preferred_element_type=jnp.float32).astype(
        jnp.bfloat16
    )
    s_ip = jnp.einsum("brk,bcpk->bcrp", rs, oh_p, preferred_element_type=jnp.float32).astype(jnp.bfloat16)
    s_qj = jnp.einsum("bcqk,bkj->bcqj", oh_q, col_s, preferred_element_type=jnp.float32).astype(jnp.bfloat16)

    summed = lax.psum_scatter(
        exchange_integral_halves[0], "aux", scatter_dimension=1, tiled=True
    )
    left_f = jnp.einsum("bra,bad->brd", f_ii, amplitudes, preferred_element_type=jnp.float32).astype(
        jnp.bfloat16
    )
    left_s = jnp.einsum("bra,bad->brd", s_ii, amplitudes, preferred_element_type=jnp.float32).astype(
        jnp.bfloat16
    )
    summed = summed + jnp.einsum("brd,bdj->brj", left_f, s_jj, preferred_element_type=jnp.float32)
    summed = summed + jnp.einsum("brd,bdj->brj", left_s, f_jj, preferred_element_type=jnp.float32)
    summed = summed - energy_sum[:, None, None] * jnp.einsum(
        "brd,bdj->brj", left_s, s_jj, preferred_element_type=jnp.float32
    )

    blocks = every_amp[global_slot]
    blocks = jnp.where(flipped[:, :, None, None], jnp.swapaxes(blocks, 2, 3), blocks)
    reach = jnp.einsum("bcrp,bcpd->bcrd", s_ip, blocks, preferred_element_type=jnp.float32).astype(
        jnp.bfloat16
    )
    for column in range(coupled_pair_owner.shape[1]):
        summed = summed - coupling_fock_element[:, column][:, None, None] * jnp.einsum(
            "brd,bdj->brj", reach[:, column], s_qj[:, column], preferred_element_type=jnp.float32
        )

    pao_energy = jnp.diagonal(pao_fock).astype(jnp.float32)
    denom = (
        pao_energy[rows_dom][:, :, None] + pao_energy[dom_j][:, None, :] - energy_sum[:, None, None]
    )
    amp_rows = lax.dynamic_slice_in_dim(amplitudes, row_first, half_rows, 1).astype(jnp.float32)
    updated = (amp_rows - summed / denom).astype(jnp.bfloat16)
    return (summed, updated)


def solution(mesh):
    placed = (
        P("aux", ("groups", "orb"), None, None),
        P(("groups", "orb"), None, None),
        P("groups", None),
        P("groups", None),
        P("groups", None),
        P("groups", None),
        P("groups"),
        P(("groups", "orb"), None),
        P(("groups", "orb"), None),
        P(("groups", "orb"), None),
        P(("groups", "orb"), None),
    )
    return jax.shard_map(
        shards,
        mesh=mesh,
        in_specs=placed,
        out_specs=(P(("groups", "orb"), "aux", None), P(("groups", "orb"), "aux", None)),
        check_vma=False,
    )
```

profile of v0, /device:TPU:0, one launch (start us, length us, event | category | flops | bytes accessed | tf_op | source)
XLA Modules:
  0.0 166.4 jit_solution(18155204422644652714)
XLA Ops:
  7.2 0.0 copy-start
  7.2 0.0 all-gather.2.cloned.1.call-start
  7.2 0.7 all-gather.2.cloned.1.call-update
  7.9 1.3 gather_fusion.2
  9.3 1.3 gather_fusion
  10.6 1.3 gather_fusion.4
  11.9 1.4 gather_fusion.1
  13.3 1.3 gather_fusion.5
  14.6 1.4 gather_fusion.3
  16.0 8.0 %gather_fusion.11 = bf16[512]{0:T(512)(128)(2,1)S(1)} fusion(bf16[512,512]{1,0:T(8,128)(2,1)} %param.16, s32[512]{0:T(512)S(1)} %bitcast.130), kind=kCustom, calls=%fused_computation.11 | custom fusion | bytes 6144 | tf_op jit(solution)/shard_map/jit(diagonal)/cond/branch_0_fun/gather | solution.py:100
  24.1 0.0 copy-start.9
  24.1 0.0 copy-start.10
  24.1 0.0 copy-start.1
  24.1 6.9 %gather_fusion.13 = f32[1024]{0:T(1024)S(1)} fusion(f32[512]{0:T(512)S(1)} %convert_element_type.73, s32[1024]{0:T(1024)S(1)} %broadcast_clamp_fusion), kind=kCustom, calls=%fused_computation.13 | custom fusion | bytes 12288 | tf_op jit(solution)/shard_map/gather | solution.py:102
  31.1 0.0 copy-start.8
  31.1 0.0 copy-start.2
  31.1 0.0 copy-start.7
  31.1 6.9 %gather_fusion.12 = f32[1024]{0:T(1024)S(1)} fusion(f32[512]{0:T(512)S(1)} %convert_element_type.73, s32[1024]{0:T(1024)S(1)} %broadcast_clamp_fusion.1), kind=kCustom, calls=%fused_computation.12 | custom fusion | bytes 12288 | tf_op jit(solution)/shard_map/gather | solution.py:102
  38.0 0.0 copy-done.9
  38.0 0.0 copy-done.10
  38.0 0.1 reshape.137
  38.1 0.0 copy-done.1
  38.1 0.8 gather_fusion.6
  38.9 0.1 reshape.159
  39.0 0.1 reshape.143
  39.0 0.8 gather_fusion.7
  39.8 0.1 reshape.146
  39.9 0.1 reshape.140
  40.0 0.0 copy-done.8
  40.0 0.1 reshape.167
  40.1 0.1 reshape.151
  40.2 0.0 copy-done.2
  40.2 0.6 gather_fusion.10
  40.8 0.6 gather_fusion.8
  41.4 0.0 copy-done.7
  41.4 0.3 slice_reduce_fusion
  41.7 0.0 copy-done
  41.7 1.7 %fusion.28.clone.5 = bf16[4,256,512,1]{2,1,3,0:T(8,128)(2,1)} fusion(s32[4,256]{1,0:T(4,128)S(1)} %gather_fusion.3, bf16[512,512]{1,0:T(8,128)(2,1)S(1)} %copy-done), kind=kOutput, calls=%fused_computation.42.clone.clone.clone.2 | convolution fusion | flops 537919488 | bytes 1576960 | tf_op jit(solution)/shard_map/kc,bjc->bkj/dot_general | solution.py:69
  43.5 1.1 fusion.40
  44.6 0.0 copy-done.6
  44.6 1.9 %fusion.41 = bf16[4,256,256]{2,1,0:T(8,128)(2,1)} fusion(s32[4,256]{1,0:T(4,128)S(1)} %gather_fusion.3, bf16[512,512]{1,0:T(8,128)(2,1)S(1)} %copy-done.6), kind=kOutput, calls=%fused_computation.66 | convolution fusion | flops 807141376 | bytes 1052672 | tf_op jit(solution)/shard_map/bjk,bak->bja/dot_general | solution.py:68
  46.5 1.9 %fusion.38 = bf16[4,256,256]{2,1,0:T(8,128)(2,1)} fusion(s32[4,256]{1,0:T(4,128)S(1)} %gather_fusion.1, bf16[512,512]{1,0:T(8,128)(2,1)S(1)} %copy-done.6), kind=kOutput, calls=%fused_computation.63 | convolution fusion | flops 807141376 | bytes 1052672 | tf_op jit(solution)/shard_map/brk,bak->bra/dot_general | solution.py:64
  48.4 1.7 %fusion.24 = bf16[4,256,512]{2,1,0:T(8,128)(2,1)} fusion(s32[4,256]{1,0:T(4,128)S(1)} %gather_fusion.1, bf16[512,512]{1,0:T(8,128)(2,1)S(1)} %copy-done), kind=kOutput, calls=%fused_computation.38 | convolution fusion | flops 537919488 | bytes 1576960 | tf_op jit(solution)/shard_map/...rk,kc->...rc/dot_general | solution.py:12
  50.2 0.0 copy-done.5
  50.2 2.0 %convolution_convert_fusion = bf16[4,256,256]{2,1,0:T(8,128)(2,1)S(1)} fusion(bf16[4,256,256]{2,1,0:T(8,128)(2,1)S(1)} %copy-done.5, bf16[4,256,512]{2,1,0:T(8,128)(2,1)} %fusion.24, s32[4,256]{1,0:T(4,128)S(1)} %gather_fusion.1), kind=kOutput, calls=%fused_computation.67 | convolution fusion | flops 403701760 | bytes 2101248 | tf_op jit(solution)/shard_map/bra,bad->brd/dot_general | solution.py:81
  52.2 1.8 %convolution_add_fusion.1 = f32[4,256,256]{2,1,0:T(8,128)S(1)} fusion(bf16[4,256,256]{2,1,0:T(8,128)(2,1)S(1)} %fusion.40, bf16[4,256,256]{2,1,0:T(8,128)(2,1)} %fusion.38, bf16[4,256,256]{2,1,0:T(8,128)(2,1)S(1)} %copy-done.5, f32[1,4,256,256]{3,2,1,0:T(8,128)} %param.11), kind=kOutput, calls=%fused_computation.62 | convolution fusion | flops 268959744 | bytes 3670016 | tf_op jit(solution)/shard_map/brd,bdj->brj/dot_general | solution.py:84
  54.0 0.0 copy-start.12
  54.1 1.4 convolution_add_fusion
  55.5 0.3 fusion.37
  55.8 0.0 copy-done.12
  55.8 4.6 %fusion.13 = bf16[4,8,256,256]{3,2,1,0:T(8,128)(2,1)} fusion(s32[4,8,256]{2,1,0:T(8,128)S(1)} %bitcast.134, bf16[4,256,512,1]{2,1,3,0:T(8,128)(2,1)S(1)} %copy-done.12), kind=kOutput, calls=%fused_computation.25 | convolution fusion | flops 2153775104 | bytes 5275648 | tf_op jit(solution)/shard_map/bcqk,bkj->bcqj/dot_general | solution.py:73
  60.4 68.1 %all-gather.2.cloned.1.call-done = bf16[128,256,256]{2,1,0:T(8,128)(2,1)} async-done(((bf16[4,256,256]{2,1,0:T(8,128)(2,1)}), bf16[128,256,256]{2,1,0:T(8,128)(2,1)}) %all-gather.2.cloned.1.call-update) | async-done | bytes 16777232 | tf_op jit(solution)/shard_map/all_gather | solution.py:38
  128.5 8.6 %gather_fusion.9 = bf16[32,256,256]{2,1,0:T(8,128)(2,1)} fusion(bf16[128,256,256]{2,1,0:T(8,128)(2,1)} %all-gather.2.cloned.1.call-done, s32[1024]{0:T(1024)S(1)} %pad_clamp_fusion.1), kind=kCustom, calls=%fused_computation.9 | custom fusion | bytes 8388736 | tf_op jit(solution)/shard_map/gather | solution.py:90
  137.0 6.3 %copy.15 = bf16[4,8,256,256]{3,2,1,0:T(8,128)(2,1)} copy(bf16[4,8,256,256]{2,3,1,0:T(8,128)(2,1)} %bitcast.131) | data formatting | bytes 8388608 | tf_op jit(solution)/shard_map/transpose | solution.py:91
  143.3 0.0 copy-done.11
  143.3 8.1 %fusion.8 = bf16[4,8,256,256]{3,2,1,0:T(8,128)(2,1)} fusion(bf16[4,8,256,256]{3,2,1,0:T(8,128)(2,1)} %copy.15, bf16[4,8,256,256]{3,2,1,0:T(8,128)(2,1)} %bitcast.132, pred[4,8]{1,0:T(4,128)(4,1)S(1)} %get-tuple-element.11, s32[4,8,256]{2,1,0:T(8,128)S(1)} %bitcast.133, bf16[4,256,512]{2,1,0:T(8,128)(2,1)S(1)} %copy-done.11), kind=kOutput, calls=%fused_computation.24 | convolution fusion | flops 3231711232 | bytes 13664288 | tf_op jit(solution)/shard_map/bcrp,bcpd->bcrd/dot_general | solution.py:92
  151.4 1.7 fusion.36
  153.1 2.3 %fusion.35 = f32[4,256,256]{2,1,0:T(8,128)S(1)} fusion(f32[4,256,256]{2,1,0:T(8,128)S(1)} %fusion.36, bf16[4,8,256,256]{3,2,1,0:T(8,128)(2,1)} %fusion.13, bf16[4,8,256,256]{3,2,1,0:T(8,128)(2,1)} %fusion.8, f32[4]{0:T(128)S(1)} %get-tuple-element.7), kind=kOutput, calls=%fused_computation.56 | convolution fusion | flops 134742016 | bytes 3145744 | tf_op jit(solution)/shard_map/brd,bdj->brj/dot_general | solution.py:96
  155.3 1.4 fusion.34
  156.7 0.3 fusion.33
  157.0 0.3 fusion.32
  157.3 0.3 fusion.31
  157.7 0.3 fusion.30
  158.0 1.6 subtract_convert_fusion
  (30 shorter events, 0.1 us)
Async XLA Ops:
  7.2 34.6 %copy-start = (bf16[512,512]{1,0:T(8,128)(2,1)S(1)}, bf16[512,512]{1,0:T(8,128)(2,1)}, u32[]{:S(2)}) copy-start(bf16[512,512]{1,0:T(8,128)(2,1)} %param.15) | copy-start | bytes 1572868
  7.2 121.3 %all-gather.2.cloned.1.call-start = ((), (), s32[]{:S(2)}) async-start(), calls=%async_computation | async-start | bytes 17301504 | tf_op jit(solution)/shard_map/all_gather | solution.py:38
  24.1 13.9 %copy-start.9 = (s32[4,8]{1,0:T(4,128)S(1)}, s32[4,8]{1,0:T(4,128)}, u32[]{:S(2)}) copy-start(s32[4,8]{1,0:T(4,128)} %param.19) | copy-start | bytes 388
  24.1 13.9 %copy-start.10 = (s32[4,8]{1,0:T(4,128)S(1)}, s32[4,8]{1,0:T(4,128)}, u32[]{:S(2)}) copy-start(s32[4,8]{1,0:T(4,128)} %param.18) | copy-start | bytes 388
  24.1 14.0 %copy-start.1 = (s32[128,2]{0,1:T(2,128)S(1)}, s32[128,2]{0,1:T(2,128)}, u32[]{:S(2)}) copy-start(s32[128,2]{0,1:T(2,128)} %param.13) | copy-start | bytes 3076
  31.1 8.9 %copy-start.8 = (s32[4,8]{1,0:T(4,128)S(1)}, s32[4,8]{1,0:T(4,128)}, u32[]{:S(2)}) copy-start(s32[4,8]{1,0:T(4,128)} %param.20) | copy-start | bytes 388
  31.1 9.1 %copy-start.2 = (s32[64,256]{1,0:T(8,128)S(1)}, s32[64,256]{1,0:T(8,128)}, u32[]{:S(2)}) copy-start(s32[64,256]{1,0:T(8,128)} %param.14) | copy-start | bytes 196612
  31.1 10.3 %copy-start.7 = (f32[4,8]{1,0:T(4,128)S(1)}, f32[4,8]{1,0:T(4,128)}, u32[]{:S(2)}) copy-start(f32[4,8]{1,0:T(4,128)} %param.21) | copy-start | bytes 388
  39.8 4.8 %copy-start.6 = (bf16[512,512]{1,0:T(8,128)(2,1)S(1)}, bf16[512,512]{1,0:T(8,128)(2,1)}, u32[]{:S(2)}) copy-start(bf16[512,512]{1,0:T(8,128)(2,1)} %param.16) | copy-start | bytes 1572868
  46.5 3.6 %copy-start.5 = (bf16[4,256,256]{2,1,0:T(8,128)(2,1)S(1)}, bf16[4,256,256]{2,1,0:T(8,128)(2,1)}, u32[]{:S(2)}) copy-start(bf16[4,256,256]{2,1,0:T(8,128)(2,1)} %param.12) | copy-start | bytes 1572868
  54.0 1.8 %copy-start.12 = (bf16[4,256,512,1]{2,1,3,0:T(8,128)(2,1)S(1)}, bf16[4,256,512,1]{2,1,3,0:T(8,128)(2,1)}, u32[]{:S(2)}) copy-start(bf16[4,256,512,1]{2,1,3,0:T(8,128)(2,1)} %fusion.28.clone.5) | copy-start | bytes 3145732
  137.0 6.3 %copy-start.11 = (bf16[4,256,512]{2,1,0:T(8,128)(2,1)S(1)}, bf16[4,256,512]{2,1,0:T(8,128)(2,1)}, u32[]{:S(2)}) copy-start(bf16[4,256,512]{2,1,0:T(8,128)(2,1)} %fusion.24) | copy-start | bytes 3145732
  151.4 3.9 %copy-start.3 = (bf16[4,8,256,256]{3,2,1,0:T(8,128)(2,1)S(1)}, bf16[4,8,256,256]{3,2,1,0:T(8,128)(2,1)}, u32[]{:S(2)}) copy-start(bf16[4,8,256,256]{3,2,1,0:T(8,128)(2,1)} %fusion.13) | copy-start | bytes 12582916
  151.4 5.3 %copy-start.4 = (bf16[4,8,256,256]{3,2,1,0:T(8,128)(2,1)S(1)}, bf16[4,8,256,256]{3,2,1,0:T(8,128)(2,1)}, u32[]{:S(2)}) copy-start(bf16[4,8,256,256]{3,2,1,0:T(8,128)(2,1)} %fusion.8) | copy-start | bytes 12582916
Sparse Core Ops, SparseCore 0:
  10.9 117.5 all-gather.1
where the time goes:
time: 167 us; the launch traced here: 166 us
  waiting for transfers between devices  68.8 us (41%)
  local copies, waits for them, and re-layouts  48.3 us (29%)
  matrix products  34.8 us (21%)
  between operations  14.4 us (9%)
    all_gather x1, waiting for transfers between devices, shards(): every_amp = lax.all_gather(amplitudes, 'orb', axis=0, tiled=True)  68.1 us
    gather x1, local copies, waits for them, and re-layouts, shards(): blocks = every_amp[global_slot]  8.55 us
    dot_general x8, matrix products, shards(): jnp.einsum('brd,bdj->brj', reach[:, column], s_qj[:, column], preferred_e...  8.1 us
    dot_general x1, matrix products, shards(): jnp.einsum('bcrp,bcpd->bcrd', s_ip, blocks, preferred_element_type=jnp.fl...  8.09 us
    gather x1, local copies, waits for them, and re-layouts, shards(): pao_energy = jnp.diagonal(pao_fock).astype(jnp.float32)  8.03 us
    gather x2, local copies, waits for them, and re-layouts, shards(): pao_energy[dom_j][:, None, :]  6.88 us
    gather x2, local copies, waits for them, and re-layouts, shards(): pao_energy[rows_dom][:, :, None] + pao_energy[dom_j][:, None, :]  6.88 us
    transpose x1, local copies, waits for them, and re-layouts, shards(): jnp.swapaxes(blocks, 2, 3)  6.29 us
  transfers between devices with their start and end apart: 1, of which 1 were waited for; matrix products, arithmetic and copies ran while one was open for 31% of the time, Pallas kernels for 0%

commit v1 on v0

--- a/solution.py
+++ b/solution.py
@@ -30,12 +30,14 @@
     slot_count, extent = amplitudes.shape[0], amplitudes.shape[1]
     paos = pao_intersection.shape[0]
     halves = lax.axis_size("aux")
-    owner_index = lax.axis_index("orb")
+    owner_index = lax.axis_index("orb_hi") * 2 + lax.axis_index("orb_lo")
     aux_index = lax.axis_index("aux")
     half_rows = extent // halves
     row_first = aux_index * half_rows
 
-    every_amp = lax.all_gather(amplitudes, "orb", axis=0, tiled=True)
+    pair_index = lax.axis_index("orb_lo")
+    mine = lax.all_gather(amplitudes, "orb_hi", axis=0, tiled=True)
+    other = lax.ppermute(mine, "orb_lo", perm=[(0, 1), (1, 0)])
 
     own_slots = owner_index * slot_count + jnp.arange(slot_count, dtype=jnp.int32)
     orb_i = pair_slot_orbitals[own_slots, 0]
@@ -87,7 +89,9 @@
         "brd,bdj->brj", left_s, s_jj, preferred_element_type=jnp.float32
     )
 
-    blocks = every_amp[global_slot]
+    local_slot = (coupled_pair_owner // 2) * slot_count + coupled_pair_slot
+    same_side = (coupled_pair_owner % 2) == pair_index
+    blocks = jnp.where(same_side[:, :, None, None], mine[local_slot], other[local_slot])
     blocks = jnp.where(flipped[:, :, None, None], jnp.swapaxes(blocks, 2, 3), blocks)
     reach = jnp.einsum("bcrp,bcpd->bcrd", s_ip, blocks, preferred_element_type=jnp.float32).astype(
         jnp.bfloat16
@@ -107,23 +111,29 @@
 
 
 def solution(mesh):
+    sizes = dict(mesh.shape)
+    split = jax.sharding.Mesh(
+        mesh.devices.reshape(sizes["groups"], sizes["orb"] // 2, 2, sizes["aux"]),
+        ("groups", "orb_hi", "orb_lo", "aux"),
+    )
+    owner = ("groups", "orb_hi", "orb_lo")
     placed = (
-        P("aux", ("groups", "orb"), None, None),
-        P(("groups", "orb"), None, None),
+        P("aux", owner, None, None),
+        P(owner, None, None),
         P("groups", None),
         P("groups", None),
         P("groups", None),
         P("groups", None),
         P("groups"),
-        P(("groups", "orb"), None),
-        P(("groups", "orb"), None),
-        P(("groups", "orb"), None),
-        P(("groups", "orb"), None),
+        P(owner, None),
+        P(owner, None),
+        P(owner, None),
+        P(owner, None),
     )
     return jax.shard_map(
         shards,
-        mesh=mesh,
+        mesh=split,
         in_specs=placed,
-        out_specs=(P(("groups", "orb"), "aux", None), P(("groups", "orb"), "aux", None)),
+        out_specs=(P(owner, "aux", None), P(owner, "aux", None)),
         check_vma=False,
     )

time: 167 us -> 225 us (1.35)
  waiting for transfers between devices: 68.8 us -> 119 us
  other arithmetic: 0.11 us -> 6.71 us
    all_gather x1, waiting for transfers between devices: 68.1 us -> 118 us  [shards(): mine = lax.all_gather(amplitudes, 'orb_hi', axis=0, tiled=True)]
    select_n x0 -> x1, local copies, waits for them, and re-layouts: none -> 6.3 us  [shards(): jnp.where(same_side[:, :, None, None], mine[local_slot], other[local_slot])]
    transpose x1 -> x0, local copies, waits for them, and re-layouts: 6.29 us -> none  [shards(): jnp.swapaxes(blocks, 2, 3)]
    select_n x0 -> x1, other arithmetic: none -> 5.89 us  [shards(): jnp.where(same_side[:, :, None, None], mine[local_slot], other[local_slot])]
    gather x1 -> x2, local copies, waits for them, and re-layouts: 8.55 us -> 12.3 us  [the longest x1 6.17 us: shards(): other[local_slot]]
    gather x1, local copies, waits for them, and re-layouts: 8.03 us -> 4.85 us  [shards(): pao_energy = jnp.diagonal(pao_fock).astype(jnp.float32)]
  transfers between devices with their start and end apart: 1 -> 2, of which waited for: 1 -> 1; matrix products, arithmetic and copies ran while one was open for 31% -> 25% of each run, Pallas kernels for 0% -> 0%
where the time goes in v1:
time: 225 us
  waiting for transfers between devices  119 us (53%)
  local copies, waits for them, and re-layouts  48.9 us (22%)
  matrix products  35.5 us (16%)
  between operations  14.4 us (6%)
  other arithmetic  6.71 us (3%)
    all_gather x1, waiting for transfers between devices, shards(): mine = lax.all_gather(amplitudes, 'orb_hi', axis=0, tiled=True)  118 us
    dot_general x1, matrix products, shards(): jnp.einsum('bcrp,bcpd->bcrd', s_ip, blocks, preferred_element_type=jnp.fl...  8.85 us
    dot_general x8, matrix products, shards(): jnp.einsum('brd,bdj->brj', reach[:, column], s_qj[:, column], preferred_e...  8.1 us
    gather x2, local copies, waits for them, and re-layouts, shards(): pao_energy[rows_dom][:, :, None] + pao_energy[dom_j][:, None, :]  6.88 us
    gather x2, local copies, waits for them, and re-layouts, shards(): pao_energy[dom_j][:, None, :]  6.88 us
    select_n x1, local copies, waits for them, and re-layouts, shards(): jnp.where(same_side[:, :, None, None], mine[local_slot], other[local_slot])  6.3 us
    gather x1, local copies, waits for them, and re-layouts, shards(): other[local_slot]  6.17 us
    gather x1, local copies, waits for them, and re-layouts, shards(): mine[local_slot]  6.16 us
  transfers between devices with their start and end apart: 2, of which 1 were waited for; matrix products, arithmetic and copies ran while one was open for 25% of the time, Pallas kernels for 0%

profile of v1, /device:TPU:0, one launch (start us, length us, event | category | flops | bytes accessed | tf_op | source)
XLA Modules:
  0.0 224.7 jit_solution(17593736677285004567)
XLA Ops:
  7.2 0.0 copy-start
  7.2 0.0 copy-start.1
  7.2 0.0 copy-start.2
  7.2 0.0 copy-start.9
  7.2 0.0 copy-start.6
  7.2 0.0 all-gather.2.cloned.1.call-start
  7.3 0.7 all-gather.2.cloned.1.call-update
  8.0 118.4 %all-gather.2.cloned.1.call-done = bf16[64,256,256]{2,1,0:T(8,128)(2,1)} async-done(((bf16[4,256,256]{2,1,0:T(8,128)(2,1)}), bf16[64,256,256]{2,1,0:T(8,128)(2,1)}) %all-gather.2.cloned.1.call-update) | async-done | bytes 8388624 | tf_op jit(solution)/shard_map/all_gather | solution.py:39
  126.4 0.0 collective-permute-start
  126.4 1.3 gather_fusion
  127.7 1.3 gather_fusion.2
  129.1 1.4 gather_fusion.1
  130.5 1.4 gather_fusion.3
  131.9 1.3 gather_fusion.4
  133.2 1.3 gather_fusion.5
  134.5 0.7 broadcast_or_fusion
  135.2 0.1 reshape.160
  135.3 0.1 reshape.138
  135.4 0.0 copy-done.1
  135.4 0.8 gather_fusion.6
  136.1 0.1 reshape.141
  136.2 0.1 reshape.144
  136.3 0.8 gather_fusion.7
  137.1 0.1 reshape.147
  137.1 0.1 reshape.152
  137.2 0.0 copy-done.2
  137.2 0.6 gather_fusion.8
  137.9 0.1 reshape.176
  138.0 0.6 gather_fusion.11
  138.6 0.0 copy-done.6
  138.6 4.8 %gather_fusion.12 = bf16[512]{0:T(512)(128)(2,1)S(1)} fusion(bf16[512,512]{1,0:T(8,128)(2,1)S(1)} %copy-done.6, s32[512]{0:T(512)S(1)} %bitcast.131), kind=kCustom, calls=%fused_computation.12 | custom fusion | bytes 6144 | tf_op jit(solution)/shard_map/jit(diagonal)/cond/branch_0_fun/gather | solution.py:104
  143.5 0.0 copy-start.7
  143.5 6.9 %gather_fusion.13 = f32[1024]{0:T(1024)S(1)} fusion(f32[512]{0:T(512)S(1)} %convert_element_type.73, s32[1024]{0:T(1024)S(1)} %broadcast_clamp_fusion.1), kind=kCustom, calls=%fused_computation.13 | custom fusion | bytes 12288 | tf_op jit(solution)/shard_map/gather | solution.py:106
  150.4 0.0 copy-start.8
  150.4 6.9 %gather_fusion.14 = f32[1024]{0:T(1024)S(1)} fusion(f32[512]{0:T(512)S(1)} %convert_element_type.73, s32[1024]{0:T(1024)S(1)} %broadcast_clamp_fusion), kind=kCustom, calls=%fused_computation.14 | custom fusion | bytes 12288 | tf_op jit(solution)/shard_map/gather | solution.py:106
  157.4 0.0 copy-done.7
  157.4 0.3 slice_reduce_fusion
  157.7 1.8 fusion.29.clone.5
  159.4 1.1 fusion.41
  160.6 1.9 fusion.39
  162.5 1.9 fusion.42
  164.4 1.7 fusion.25
  166.1 0.0 copy-done.5
  166.1 2.0 convolution_convert_fusion
  168.1 1.8 convolution_add_fusion.1
  170.0 1.4 convolution_add_fusion
  171.4 0.3 fusion.38
  171.7 0.0 copy-done.11
  171.8 4.6 %fusion.13 = bf16[4,8,256,256]{3,2,1,0:T(8,128)(2,1)} fusion(s32[4,8,256]{2,1,0:T(8,128)S(1)} %bitcast.137, bf16[4,256,512,1]{2,1,3,0:T(8,128)(2,1)S(1)} %copy-done.11), kind=kOutput, calls=%fused_computation.27 | convolution fusion | flops 2153775104 | bytes 5275648 | tf_op jit(solution)/shard_map/bcqk,bkj->bcqj/dot_general | solution.py:75
  176.3 6.2 %gather_fusion.9 = bf16[32,256,256]{2,1,0:T(8,128)(2,1)} fusion(bf16[64,256,256]{2,1,0:T(8,128)(2,1)} %all-gather.2.cloned.1.call-done, s32[1024]{0:T(1024)S(1)} %pad_clamp_fusion.1), kind=kCustom, calls=%fused_computation.9 | custom fusion | bytes 8388736 | tf_op jit(solution)/shard_map/gather | solution.py:94
  182.5 0.0 collective-permute-done
  182.5 6.2 %gather_fusion.10 = bf16[32,256,256]{2,1,0:T(8,128)(2,1)} fusion(bf16[64,256,256]{2,1,0:T(8,128)(2,1)} %collective-permute-done, s32[1024]{0:T(1024)S(1)} %pad_clamp_fusion.1), kind=kCustom, calls=%fused_computation.10 | custom fusion | bytes 8388736 | tf_op jit(solution)/shard_map/gather | solution.py:94
  188.7 5.9 %fusion.23 = bf16[4,8,256,256]{2,3,1,0:T(8,128)(2,1)} fusion(bf16[4,8,256,256]{3,2,1,0:T(8,128)(2,1)} %bitcast.132, bf16[4,8,256,256]{3,2,1,0:T(8,128)(2,1)} %bitcast.134, pred[4,8]{1,0:T(4,128)(4,1)S(1)} %fusion.66), kind=kLoop, calls=%fused_computation.39 | loop fusion | flops 2097152 | bytes 12582944 | tf_op jit(solution)/shard_map/jit(_where)/select_n | solution.py:94
  194.5 6.3 %copy.15 = bf16[4,8,256,256]{3,2,1,0:T(8,128)(2,1)} copy(bf16[4,8,256,256]{2,3,1,0:T(8,128)(2,1)} %fusion.23) | data formatting | bytes 8388608 | tf_op jit(solution)/shard_map/jit(_where)/select_n | solution.py:94
  200.8 8.9 %fusion.8 = bf16[4,8,256,256]{3,2,1,0:T(8,128)(2,1)} fusion(bf16[4,8,256,256]{3,2,1,0:T(8,128)(2,1)} %copy.15, pred[4,8]{1,0:T(4,128)(4,1)S(1)} %get-tuple-element.11, s32[4,8,256]{2,1,0:T(8,128)S(1)} %bitcast.136, bf16[4,8,256,256]{3,2,1,0:T(8,128)(2,1)} %bitcast.133, bf16[4,8,256,256]{3,2,1,0:T(8,128)(2,1)} %bitcast.135, pred[4,8]{1,0:T(4,128)(4,1)S(1)} %fusion.66, ...), kind=kOutput, calls=%fused_computation.26 | convolution fusion | flops 3233808384 | bytes 17858624 | tf_op jit(solution)/shard_map/bcrp,bcpd->bcrd/dot_general | solution.py:96
  209.7 1.7 fusion.37
  211.4 2.3 %fusion.36 = f32[4,256,256]{2,1,0:T(8,128)S(1)} fusion(f32[4,256,256]{2,1,0:T(8,128)S(1)} %fusion.37, bf16[4,8,256,256]{3,2,1,0:T(8,128)(2,1)} %fusion.13, bf16[4,8,256,256]{3,2,1,0:T(8,128)(2,1)} %fusion.8, f32[4]{0:T(128)S(1)} %get-tuple-element.7), kind=kOutput, calls=%fused_computation.59 | convolution fusion | flops 134742016 | bytes 3145744 | tf_op jit(solution)/shard_map/brd,bdj->brj/dot_general | solution.py:100
  213.6 1.4 fusion.35
  215.0 0.0 copy-done.4
  215.0 0.3 fusion.34
  215.3 0.3 fusion.33
  215.7 0.3 fusion.32
  216.0 0.3 fusion.31
  216.3 1.6 subtract_convert_fusion
  (32 shorter events, 0.2 us)
Async XLA Ops:
  7.2 150.5 %copy-start = (bf16[512,512]{1,0:T(8,128)(2,1)S(1)}, bf16[512,512]{1,0:T(8,128)(2,1)}, u32[]{:S(2)}) copy-start(bf16[512,512]{1,0:T(8,128)(2,1)} %param.15) | copy-start | bytes 1572868
  7.2 128.2 %copy-start.1 = (s32[128,2]{0,1:T(2,128)S(1)}, s32[128,2]{0,1:T(2,128)}, u32[]{:S(2)}) copy-start(s32[128,2]{0,1:T(2,128)} %param.13) | copy-start | bytes 3076
  7.2 130.1 %copy-start.2 = (s32[64,256]{1,0:T(8,128)S(1)}, s32[64,256]{1,0:T(8,128)}, u32[]{:S(2)}) copy-start(s32[64,256]{1,0:T(8,128)} %param.14) | copy-start | bytes 196612
  7.2 129.9 %copy-start.9 = (s32[4,8]{1,0:T(4,128)S(1)}, s32[4,8]{1,0:T(4,128)}, u32[]{:S(2)}) copy-start(s32[4,8]{1,0:T(4,128)} %param.20) | copy-start | bytes 388
  7.2 131.4 %copy-start.6 = (bf16[512,512]{1,0:T(8,128)(2,1)S(1)}, bf16[512,512]{1,0:T(8,128)(2,1)}, u32[]{:S(2)}) copy-start(bf16[512,512]{1,0:T(8,128)(2,1)} %param.16) | copy-start | bytes 1572868
  7.2 119.2 %all-gather.2.cloned.1.call-start = ((), (), s32[]{:S(2)}) async-start(), calls=%async_computation | async-start | bytes 8912896 | tf_op jit(solution)/shard_map/all_gather | solution.py:39
  126.4 56.1 %collective-permute-start = (bf16[64,256,256]{2,1,0:T(8,128)(2,1)}, bf16[64,256,256]{2,1,0:T(8,128)(2,1)}, u32[]{:S(2)}, u32[]{:S(2)}) collective-permute-start(bf16[64,256,256]{2,1,0:T(8,128)(2,1)} %all-gather.2.cloned.1.call-done), channel_id=1, source_target_pairs={{0,1},{1,0},{2,3},{3,2},{4,5},{5,4},{6,7},{7,6},{8,9},{9,8},{10,11... | collective-permute-start | bytes 25165832 | tf_op jit(solution)/shard_map/ppermute | solution.py:40
  143.5 13.9 %copy-start.7 = (f32[4,8]{1,0:T(4,128)S(1)}, f32[4,8]{1,0:T(4,128)}, u32[]{:S(2)}) copy-start(f32[4,8]{1,0:T(4,128)} %param.21) | copy-start | bytes 388
  150.4 9.0 %copy-start.8 = (s32[4,8]{1,0:T(4,128)S(1)}, s32[4,8]{1,0:T(4,128)}, u32[]{:S(2)}) copy-start(s32[4,8]{1,0:T(4,128)} %param.18) | copy-start | bytes 388
  162.5 3.7 %copy-start.5 = (bf16[4,256,256]{2,1,0:T(8,128)(2,1)S(1)}, bf16[4,256,256]{2,1,0:T(8,128)(2,1)}, u32[]{:S(2)}) copy-start(bf16[4,256,256]{2,1,0:T(8,128)(2,1)} %param.12) | copy-start | bytes 1572868
  170.0 1.8 copy-start.11
  194.5 6.3 %copy-start.10 = (bf16[4,256,512]{2,1,0:T(8,128)(2,1)S(1)}, bf16[4,256,512]{2,1,0:T(8,128)(2,1)}, u32[]{:S(2)}) copy-start(bf16[4,256,512]{2,1,0:T(8,128)(2,1)} %fusion.25) | copy-start | bytes 3145732
  209.7 3.9 %copy-start.3 = (bf16[4,8,256,256]{3,2,1,0:T(8,128)(2,1)S(1)}, bf16[4,8,256,256]{3,2,1,0:T(8,128)(2,1)}, u32[]{:S(2)}) copy-start(bf16[4,8,256,256]{3,2,1,0:T(8,128)(2,1)} %fusion.13) | copy-start | bytes 12582916
  209.7 5.3 %copy-start.4 = (bf16[4,8,256,256]{3,2,1,0:T(8,128)(2,1)S(1)}, bf16[4,8,256,256]{3,2,1,0:T(8,128)(2,1)}, u32[]{:S(2)}) copy-start(bf16[4,8,256,256]{3,2,1,0:T(8,128)(2,1)} %fusion.8) | copy-start | bytes 12582916
Sparse Core Ops, SparseCore 0:
  10.8 115.5 all-gather.1

commit v2 on v0

--- a/solution.py
+++ b/solution.py
@@ -1,6 +1,8 @@
 import jax
 import jax.numpy as jnp
 from jax import lax
+from jax.experimental import pallas as pl
+from jax.experimental.pallas import tpu as pltpu
 from jax.sharding import PartitionSpec as P
 
 
@@ -12,6 +14,83 @@
     return jnp.einsum(
         "...rk,kc->...rc", onehot, matrix, preferred_element_type=jnp.float32
     ).astype(jnp.bfloat16)
+
+
+def coupling_kernel(
+    slot_ref, flip_ref, fock_ref, blk_ref, sip_ref, sqj_ref, own_ref, den_ref, amp_ref, res_ref, upd_ref, reach
+):
+    b, c = pl.program_id(0), pl.program_id(1)
+    couplings = pl.num_programs(1)
+    at = b * couplings + c
+
+    @pl.when(c == 0)
+    def _():
+        res_ref[...] = own_ref[...]
+
+    @pl.when(flip_ref[at] == 1)
+    def _():
+        reach[...] = lax.dot_general(
+            sip_ref[...], blk_ref[...], (((1,), (1,)), ((), ())), preferred_element_type=jnp.float32
+        ).astype(jnp.bfloat16)
+
+    @pl.when(flip_ref[at] != 1)
+    def _():
+        reach[...] = jnp.dot(sip_ref[...], blk_ref[...], preferred_element_type=jnp.float32).astype(
+            jnp.bfloat16
+        )
+
+    res_ref[...] = res_ref[...] - fock_ref[at] * jnp.dot(
+        reach[...], sqj_ref[...], preferred_element_type=jnp.float32
+    )
+
+    @pl.when(c == couplings - 1)
+    def _():
+        upd_ref[...] = (amp_ref[...].astype(jnp.float32) - res_ref[...] / den_ref[...]).astype(jnp.bfloat16)
+
+
+def couple_and_update(every_amp, global_slot, flipped, fock, s_ip, s_qj, own, denom, amp_rows):
+    slots, couplings = global_slot.shape
+    rows, cols = own.shape[1], own.shape[2]
+    extent = every_amp.shape[1]
+    grid_spec = pltpu.PrefetchScalarGridSpec(
+        num_scalar_prefetch=3,
+        grid=(slots, couplings),
+        in_specs=[
+            pl.BlockSpec((None, extent, extent), lambda b, c, gs, fl, fe: (gs[b * couplings + c], 0, 0)),
+            pl.BlockSpec((None, None, rows, extent), lambda b, c, gs, fl, fe: (b, c, 0, 0)),
+            pl.BlockSpec((None, None, extent, cols), lambda b, c, gs, fl, fe: (b, c, 0, 0)),
+            pl.BlockSpec((None, rows, cols), lambda b, c, gs, fl, fe: (b, 0, 0)),
+            pl.BlockSpec((None, rows, cols), lambda b, c, gs, fl, fe: (b, 0, 0)),
+            pl.BlockSpec((None, rows, cols), lambda b, c, gs, fl, fe: (b, 0, 0)),
+        ],
+        out_specs=[
+            pl.BlockSpec((None, rows, cols), lambda b, c, gs, fl, fe: (b, 0, 0)),
+            pl.BlockSpec((None, rows, cols), lambda b, c, gs, fl, fe: (b, 0, 0)),
+        ],
+        scratch_shapes=[pltpu.VMEM((rows, extent), jnp.bfloat16)],
+    )
+    flops = 4 * slots * couplings * rows * extent * extent
+    moved = slots * couplings * (extent * extent * 2 + rows * extent * 2 + extent * cols * 2) + slots * rows * cols * 18
+    return pl.pallas_call(
+        coupling_kernel,
+        grid_spec=grid_spec,
+        out_shape=[
+            jax.ShapeDtypeStruct(own.shape, jnp.float32),
+            jax.ShapeDtypeStruct(own.shape, jnp.bfloat16),
+        ],
+        compiler_params=pltpu.CompilerParams(dimension_semantics=("arbitrary", "arbitrary")),
+        cost_estimate=pl.CostEstimate(flops=flops, bytes_accessed=moved, transcendentals=0),
+    )(
+        global_slot.reshape(-1),
+        flipped.astype(jnp.int32).reshape(-1),
+        fock.reshape(-1),
+        every_amp,
+        s_ip,
+        s_qj,
+        own,
+        denom,
+        amp_rows,
+    )
 
 
 def shards(
@@ -87,23 +166,14 @@
         "brd,bdj->brj", left_s, s_jj, preferred_element_type=jnp.float32
     )
 
-    blocks = every_amp[global_slot]
-    blocks = jnp.where(flipped[:, :, None, None], jnp.swapaxes(blocks, 2, 3), blocks)
-    reach = jnp.einsum("bcrp,bcpd->bcrd", s_ip, blocks, preferred_element_type=jnp.float32).astype(
-        jnp.bfloat16
-    )
-    for column in range(coupled_pair_owner.shape[1]):
-        summed = summed - coupling_fock_element[:, column][:, None, None] * jnp.einsum(
-            "brd,bdj->brj", reach[:, column], s_qj[:, column], preferred_element_type=jnp.float32
-        )
-
     pao_energy = jnp.diagonal(pao_fock).astype(jnp.float32)
     denom = (
         pao_energy[rows_dom][:, :, None] + pao_energy[dom_j][:, None, :] - energy_sum[:, None, None]
     )
-    amp_rows = lax.dynamic_slice_in_dim(amplitudes, row_first, half_rows, 1).astype(jnp.float32)
-    updated = (amp_rows - summed / denom).astype(jnp.bfloat16)
-    return (summed, updated)
+    amp_rows = lax.dynamic_slice_in_dim(amplitudes, row_first, half_rows, 1)
+    return couple_and_update(
+        every_amp, global_slot, flipped, coupling_fock_element, s_ip, s_qj, summed, denom, amp_rows
+    )
 
 
 def solution(mesh):

time: 167 us -> 162 us (0.970)
  Pallas kernels: 0 us -> 26.3 us
  local copies, waits for them, and re-layouts: 48.3 us -> 30.3 us
  matrix products: 34.8 us -> 22.8 us
  waiting for transfers between devices: 68.8 us -> 66.5 us
    pallas_call x0 -> x1, Pallas kernels: none -> 26.3 us  [couple_and_update(): pl.pallas_call(coupling_kernel, grid_spec=grid_spec, out_shape=[jax.Shape...]
    dot_general x9 -> x1, matrix products: 16.2 us -> 5.48 us  [shards(): jnp.einsum('brk,bcpk->bcrp', rs, oh_p, preferred_element_type=jnp.float32)]
    gather x1 -> x0, local copies, waits for them, and re-layouts: 8.55 us -> none  [shards(): blocks = every_amp[global_slot]]
    transpose x1 -> x0, local copies, waits for them, and re-layouts: 6.29 us -> none  [shards(): jnp.swapaxes(blocks, 2, 3)]
    gather x1, local copies, waits for them, and re-layouts: 8.03 us -> 4.82 us  [shards(): pao_energy = jnp.diagonal(pao_fock).astype(jnp.float32)]
    all_gather x1, waiting for transfers between devices: 68.1 us -> 65.8 us  [shards(): every_amp = lax.all_gather(amplitudes, 'orb', axis=0, tiled=True)]
    reshape x0 -> x3, local copies, waits for them, and re-layouts: none -> 1.83 us  [the longest x1 0.62 us: couple_and_update(): flipped.astype(jnp.int32).reshape(-1)]
  transfers between devices with their start and end apart: 1 -> 1, of which waited for: 1 -> 1; matrix products, arithmetic and copies ran while one was open for 31% -> 33% of each run, Pallas kernels for 0% -> 0%
where the time goes in v2:
time: 162 us
  waiting for transfers between devices  66.5 us (41%)
  local copies, waits for them, and re-layouts  30.3 us (19%)
  Pallas kernels  26.3 us (16%)
  matrix products  22.8 us (14%)
  between operations  14.3 us (9%)
    all_gather x1, waiting for transfers between devices, shards(): every_amp = lax.all_gather(amplitudes, 'orb', axis=0, tiled=True)  65.8 us
    pallas_call x1, Pallas kernels, couple_and_update(): pl.pallas_call(coupling_kernel, grid_spec=grid_spec, out_shape=[jax.Shape...  26.3 us
    gather x2, local copies, waits for them, and re-layouts, shards(): pao_energy[dom_j][:, None, :]  6.87 us
    gather x2, local copies, waits for them, and re-layouts, shards(): pao_energy[rows_dom][:, :, None] + pao_energy[dom_j][:, None, :]  6.87 us
    dot_general x1, matrix products, shards(): jnp.einsum('brk,bcpk->bcrp', rs, oh_p, preferred_element_type=jnp.float32)  5.48 us
    gather x1, local copies, waits for them, and re-layouts, shards(): pao_energy = jnp.diagonal(pao_fock).astype(jnp.float32)  4.82 us
    dot_general x1, matrix products, shards(): jnp.einsum('bcqk,bkj->bcqj', oh_q, col_s, preferred_element_type=jnp.floa...  4.58 us
  transfers between devices with their start and end apart: 1, of which 1 were waited for; matrix products, arithmetic and copies ran while one was open for 33% of the time, Pallas kernels for 0%

profile of v2, /device:TPU:0, one launch (start us, length us, event | category | flops | bytes accessed | tf_op | source)
XLA Modules:
  0.0 161.7 jit_solution(1663623947542521192)
XLA Ops:
  7.2 0.0 copy-start
  7.2 0.0 copy-start.2
  7.2 0.0 copy-start.3
  7.2 0.0 copy-start.7
  7.2 0.0 copy-start.5
  7.2 0.0 all-gather.2.cloned.1.call-start
  7.3 0.7 all-gather.2.cloned.1.call-update
  8.0 1.3 gather_fusion.6
  9.3 1.3 gather_fusion.3
  10.6 1.3 gather_fusion.8
  11.9 0.0 copy-done.3
  11.9 0.6 gather_fusion.4
  12.5 0.0 copy-done.2
  12.5 0.6 gather_fusion.9
  13.2 0.6 gather_fusion.7
  13.7 0.0 copy-done.7
  13.8 0.6 reshape.98.fock_ref
  14.4 0.0 copy-done.5
  14.4 4.8 %gather_fusion.10 = bf16[512]{0:T(512)(128)(2,1)S(1)} fusion(bf16[512,512]{1,0:T(8,128)(2,1)S(1)} %copy-done.5, s32[512]{0:T(512)S(1)} %bitcast.76), kind=kCustom, calls=%fused_computation.10 | custom fusion | bytes 6144 | tf_op jit(solution)/shard_map/jit(diagonal)/cond/branch_0_fun/gather | solution.py:169
  19.2 6.9 %gather_fusion.12 = f32[1024]{0:T(1024)S(1)} fusion(f32[512]{0:T(512)S(1)} %convert_element_type.65, s32[1024]{0:T(1024)S(1)} %broadcast_clamp_fusion), kind=kCustom, calls=%fused_computation.12 | custom fusion | bytes 12288 | tf_op jit(solution)/shard_map/gather | solution.py:171
  26.1 0.0 copy-start.8
  26.2 0.0 copy-start.9
  26.2 0.0 copy-start.1
  26.2 6.9 %gather_fusion.11 = f32[1024]{0:T(1024)S(1)} fusion(f32[512]{0:T(512)S(1)} %convert_element_type.65, s32[1024]{0:T(1024)S(1)} %broadcast_clamp_fusion.1), kind=kCustom, calls=%fused_computation.11 | custom fusion | bytes 12288 | tf_op jit(solution)/shard_map/gather | solution.py:171
  33.1 0.0 copy-done.8
  33.1 0.0 copy-done.9
  33.1 0.1 reshape.107
  33.2 0.0 copy-done.1
  33.2 0.0 copy-start.6
  33.2 0.8 gather_fusion.1
  33.9 0.6 reshape.95.slot_ref
  34.6 0.1 reshape.101
  34.6 0.8 gather_fusion
  35.4 0.1 reshape.104
  35.5 0.1 reshape.110
  35.6 0.0 copy-done.6
  35.6 0.1 reshape.115
  35.7 0.1 reshape.137
  35.8 0.6 reshape.100.flip_ref
  36.4 0.6 gather_fusion.2
  37.0 0.6 gather_fusion.5
  37.6 0.0 copy-done
  37.6 1.7 %fusion.19.clone.5 = bf16[4,256,512,1]{2,1,3,0:T(8,128)(2,1)} fusion(s32[4,256]{1,0:T(4,128)S(1)} %gather_fusion.7, bf16[512,512]{1,0:T(8,128)(2,1)S(1)} %copy-done), kind=kOutput, calls=%fused_computation.37.clone.clone.clone.2 | convolution fusion | flops 537919488 | bytes 1576960 | tf_op jit(solution)/shard_map/kc,bjc->bkj/dot_general | solution.py:148
  39.4 1.1 fusion.23
  40.5 1.9 %fusion.24 = bf16[4,256,256]{2,1,0:T(8,128)(2,1)} fusion(s32[4,256]{1,0:T(4,128)S(1)} %gather_fusion.7, bf16[512,512]{1,0:T(8,128)(2,1)S(1)} %copy-done.5), kind=kOutput, calls=%fused_computation.45 | convolution fusion | flops 807141376 | bytes 1052672 | tf_op jit(solution)/shard_map/bjk,bak->bja/dot_general | solution.py:147
  42.4 1.9 %fusion.21 = bf16[4,256,256]{2,1,0:T(8,128)(2,1)} fusion(s32[4,256]{1,0:T(4,128)S(1)} %gather_fusion.4, bf16[512,512]{1,0:T(8,128)(2,1)S(1)} %copy-done.5), kind=kOutput, calls=%fused_computation.42 | convolution fusion | flops 807141376 | bytes 1052672 | tf_op jit(solution)/shard_map/brk,bak->bra/dot_general | solution.py:143
  44.3 0.0 copy-start.4
  44.3 1.3 add_subtract_fusion.den_ref
  45.6 0.8 fusion.14
  46.4 0.0 copy-start.10
  46.4 1.0 copy-done.10
  47.3 0.0 copy-done.4
  47.3 0.8 convolution_convert_fusion
  48.1 1.8 %convolution_add_fusion.1 = f32[4,256,256]{2,1,0:T(8,128)S(1)} fusion(bf16[4,256,256]{2,1,0:T(8,128)(2,1)S(1)} %fusion.23, bf16[4,256,256]{2,1,0:T(8,128)(2,1)} %fusion.21, bf16[4,256,256]{2,1,0:T(8,128)(2,1)S(1)} %copy-done.4, f32[1,4,256,256]{3,2,1,0:T(8,128)} %param.11), kind=kOutput, calls=%fused_computation.41 | convolution fusion | flops 268959744 | bytes 3670016 | tf_op jit(solution)/shard_map/brd,bdj->brj/dot_general | solution.py:163
  50.0 1.3 convolution_add_fusion
  51.3 0.0 copy-start.12
  51.3 1.3 fusion.20.own_ref
  52.6 0.0 copy-done.12
  52.6 0.0 copy-start.11
  52.6 4.6 %fusion.4.sqj_ref = bf16[4,8,256,256]{3,2,1,0:T(8,128)(2,1)} fusion(s32[4,8,256]{2,1,0:T(8,128)S(1)} %bitcast.78, bf16[4,256,512,1]{2,1,3,0:T(8,128)(2,1)S(1)} %copy-done.12), kind=kOutput, calls=%fused_computation.20 | convolution fusion | flops 2153775104 | bytes 5275648 | tf_op jit(solution)/shard_map/bcqk,bkj->bcqj/dot_general | solution.py:152
  57.2 0.0 copy-done.11
  57.2 5.5 %convert_bitcast_fusion.sip_ref = bf16[4,8,256,256]{3,2,1,0:T(8,128)(2,1)} fusion(s32[4,8,256]{2,1,0:T(8,128)S(1)} %bitcast.77, bf16[4,256,512]{2,1,0:T(8,128)(2,1)S(1)} %copy-done.11), kind=kOutput, calls=%fused_computation.19 | convolution fusion | flops 2153775104 | bytes 5275648 | tf_op jit(solution)/shard_map/brk,bcpk->bcrp/dot_general | solution.py:151
  62.7 65.8 %all-gather.2.cloned.1.call-done.blk_ref = bf16[128,256,256]{2,1,0:T(8,128)(2,1)} async-done(((bf16[4,256,256]{2,1,0:T(8,128)(2,1)}), bf16[128,256,256]{2,1,0:T(8,128)(2,1)}) %all-gather.2.cloned.1.call-update) | async-done | bytes 16777232 | tf_op jit(solution)/shard_map/all_gather | solution.py:117
  128.5 26.3 %shard_map.122 = (f32[4,256,256]{2,1,0:T(8,128)}, bf16[4,256,256]{2,1,0:T(8,128)(2,1)}) custom-call(s32[32]{0:T(128)} %reshape.95.slot_ref, s32[32]{0:T(128)} %reshape.100.flip_ref, f32[32]{0:T(128)} %reshape.98.fock_ref, bf16[128,256,256]{2,1,0:T(8,128)(2,1)} %all-gather.2.cloned.1.call-done.blk_ref, bf16[4,8,256,256]{3,2,1,0:T(8,128)(2,1)} %convert_bitcast_fusion.sip_ref, ...), custom_call_target="tpu_custom_call" | custom-call | flops 2147483648 | bytes 17301504 | tf_op jit(solution)/shard_map/pallas_call | solution.py:74
  (23 shorter events, 0.1 us)
Async XLA Ops:
  7.2 30.5 %copy-start = (bf16[512,512]{1,0:T(8,128)(2,1)S(1)}, bf16[512,512]{1,0:T(8,128)(2,1)}, u32[]{:S(2)}) copy-start(bf16[512,512]{1,0:T(8,128)(2,1)} %param.15) | copy-start | bytes 1572868
  7.2 5.4 %copy-start.2 = (f32[64]{0:T(128)S(1)}, f32[64]{0:T(128)}, u32[]{:S(2)}) copy-start(f32[64]{0:T(128)} %param.17) | copy-start | bytes 772
  7.2 4.7 %copy-start.3 = (s32[64,256]{1,0:T(8,128)S(1)}, s32[64,256]{1,0:T(8,128)}, u32[]{:S(2)}) copy-start(s32[64,256]{1,0:T(8,128)} %param.14) | copy-start | bytes 196612
  7.2 6.5 %copy-start.7 = (f32[4,8]{1,0:T(4,128)S(1)}, f32[4,8]{1,0:T(4,128)}, u32[]{:S(2)}) copy-start(f32[4,8]{1,0:T(4,128)} %param.21) | copy-start | bytes 388
  7.2 7.1 %copy-start.5 = (bf16[512,512]{1,0:T(8,128)(2,1)S(1)}, bf16[512,512]{1,0:T(8,128)(2,1)}, u32[]{:S(2)}) copy-start(bf16[512,512]{1,0:T(8,128)(2,1)} %param.16) | copy-start | bytes 1572868
  7.2 121.3 %all-gather.2.cloned.1.call-start = ((), (), s32[]{:S(2)}) async-start(), calls=%async_computation | async-start | bytes 17301504 | tf_op jit(solution)/shard_map/all_gather | solution.py:117
  26.1 6.9 %copy-start.8 = (s32[4,8]{1,0:T(4,128)S(1)}, s32[4,8]{1,0:T(4,128)}, u32[]{:S(2)}) copy-start(s32[4,8]{1,0:T(4,128)} %param.19) | copy-start | bytes 388
  26.2 6.9 %copy-start.9 = (s32[4,8]{1,0:T(4,128)S(1)}, s32[4,8]{1,0:T(4,128)}, u32[]{:S(2)}) copy-start(s32[4,8]{1,0:T(4,128)} %param.18) | copy-start | bytes 388
  26.2 7.0 %copy-start.1 = (s32[128,2]{0,1:T(2,128)S(1)}, s32[128,2]{0,1:T(2,128)}, u32[]{:S(2)}) copy-start(s32[128,2]{0,1:T(2,128)} %param.13) | copy-start | bytes 3076
  33.2 2.4 %copy-start.6 = (s32[4,8]{1,0:T(4,128)S(1)}, s32[4,8]{1,0:T(4,128)}, u32[]{:S(2)}) copy-start(s32[4,8]{1,0:T(4,128)} %param.20) | copy-start | bytes 388
  44.3 3.0 %copy-start.4 = (bf16[4,256,256]{2,1,0:T(8,128)(2,1)S(1)}, bf16[4,256,256]{2,1,0:T(8,128)(2,1)}, u32[]{:S(2)}) copy-start(bf16[4,256,256]{2,1,0:T(8,128)(2,1)} %amp_ref) | copy-start | bytes 1572868
  46.4 1.0 copy-start.10
  51.3 1.3 copy-start.12
  52.6 4.6 %copy-start.11 = (bf16[4,256,512]{2,1,0:T(8,128)(2,1)S(1)}, bf16[4,256,512]{2,1,0:T(8,128)(2,1)}, u32[]{:S(2)}) copy-start(bf16[4,256,512]{2,1,0:T(8,128)(2,1)} %copy-done.10) | copy-start | bytes 3145732
Sparse Core Ops, SparseCore 0:
  10.9 117.5 all-gather.1

commit v3 on v2

--- a/solution.py
+++ b/solution.py
@@ -1,3 +1,5 @@
+import functools
+
 import jax
 import jax.numpy as jnp
 from jax import lax
@@ -16,63 +18,74 @@
     ).astype(jnp.bfloat16)
 
 
-def coupling_kernel(
-    slot_ref, flip_ref, fock_ref, blk_ref, sip_ref, sqj_ref, own_ref, den_ref, amp_ref, res_ref, upd_ref, reach
-):
-    b, c = pl.program_id(0), pl.program_id(1)
-    couplings = pl.num_programs(1)
-    at = b * couplings + c
-
-    @pl.when(c == 0)
+def coupling_kernel(group, slot_ref, flip_ref, fock_ref, *refs):
+    blk_refs = refs[:group]
+    sip_ref, sqj_ref, own_ref, den_ref, amp_ref, res_ref, upd_ref, reach = refs[group:]
+    b, step = pl.program_id(0), pl.program_id(1)
+    steps = pl.num_programs(1)
+
+    @pl.when(step == 0)
     def _():
         res_ref[...] = own_ref[...]
 
-    @pl.when(flip_ref[at] == 1)
+    total = res_ref[...]
+    for k in range(group):
+        at = (b * steps + step) * group + k
+
+        @pl.when(flip_ref[at] == 1)
+        def _():
+            reach[...] = lax.dot_general(
+                sip_ref[k], blk_refs[k][...], (((1,), (1,)), ((), ())), preferred_element_type=jnp.float32
+            ).astype(jnp.bfloat16)
+
+        @pl.when(flip_ref[at] != 1)
+        def _():
+            reach[...] = jnp.dot(sip_ref[k], blk_refs[k][...], preferred_element_type=jnp.float32).astype(
+                jnp.bfloat16
+            )
+
+        total = total - fock_ref[at] * jnp.dot(reach[...], sqj_ref[k], preferred_element_type=jnp.float32)
+    res_ref[...] = total
+
+    @pl.when(step == steps - 1)
     def _():
-        reach[...] = lax.dot_general(
-            sip_ref[...], blk_ref[...], (((1,), (1,)), ((), ())), preferred_element_type=jnp.float32
-        ).astype(jnp.bfloat16)
-
-    @pl.when(flip_ref[at] != 1)
-    def _():
-        reach[...] = jnp.dot(sip_ref[...], blk_ref[...], preferred_element_type=jnp.float32).astype(
-            jnp.bfloat16
-        )
-
-    res_ref[...] = res_ref[...] - fock_ref[at] * jnp.dot(
-        reach[...], sqj_ref[...], preferred_element_type=jnp.float32
-    )
-
-    @pl.when(c == couplings - 1)
-    def _():
-        upd_ref[...] = (amp_ref[...].astype(jnp.float32) - res_ref[...] / den_ref[...]).astype(jnp.bfloat16)
-
-
-def couple_and_update(every_amp, global_slot, flipped, fock, s_ip, s_qj, own, denom, amp_rows):
+        upd_ref[...] = (amp_ref[...].astype(jnp.float32) - total / den_ref[...]).astype(jnp.bfloat16)
+
+
+def couple_and_update(every_amp, global_slot, flipped, fock, s_ip, s_qj, own, denom, amp_rows, group=4):
     slots, couplings = global_slot.shape
+    group = group if couplings % group == 0 else 1
+    steps = couplings // group
     rows, cols = own.shape[1], own.shape[2]
     extent = every_amp.shape[1]
+
+    def block_spec(k):
+        return pl.BlockSpec(
+            (None, extent, extent), lambda b, t, gs, fl, fe: (gs[(b * steps + t) * group + k], 0, 0)
+        )
+
+    per_slot = lambda b, t, gs, fl, fe: (b, 0, 0)
     grid_spec = pltpu.PrefetchScalarGridSpec(
         num_scalar_prefetch=3,
-        grid=(slots, couplings),
-        in_specs=[
-            pl.BlockSpec((None, extent, extent), lambda b, c, gs, fl, fe: (gs[b * couplings + c], 0, 0)),
-            pl.BlockSpec((None, None, rows, extent), lambda b, c, gs, fl, fe: (b, c, 0, 0)),
-            pl.BlockSpec((None, None, extent, cols), lambda b, c, gs, fl, fe: (b, c, 0, 0)),
-            pl.BlockSpec((None, rows, cols), lambda b, c, gs, fl, fe: (b, 0, 0)),
-            pl.BlockSpec((None, rows, cols), lambda b, c, gs, fl, fe: (b, 0, 0)),
-            pl.BlockSpec((None, rows, cols), lambda b, c, gs, fl, fe: (b, 0, 0)),
+        grid=(slots, steps),
+        in_specs=[block_spec(k) for k in range(group)]
+        + [
+            pl.BlockSpec((None, group, rows, extent), lambda b, t, gs, fl, fe: (b, t, 0, 0)),
+            pl.BlockSpec((None, group, extent, cols), lambda b, t, gs, fl, fe: (b, t, 0, 0)),
+            pl.BlockSpec((None, rows, cols), per_slot),
+            pl.BlockSpec((None, rows, cols), per_slot),
+            pl.BlockSpec((None, rows, cols), per_slot),
         ],
         out_specs=[
-            pl.BlockSpec((None, rows, cols), lambda b, c, gs, fl, fe: (b, 0, 0)),
-            pl.BlockSpec((None, rows, cols), lambda b, c, gs, fl, fe: (b, 0, 0)),
+            pl.BlockSpec((None, rows, cols), per_slot),
+            pl.BlockSpec((None, rows, cols), per_slot),
         ],
         scratch_shapes=[pltpu.VMEM((rows, extent), jnp.bfloat16)],
     )
     flops = 4 * slots * couplings * rows * extent * extent
     moved = slots * couplings * (extent * extent * 2 + rows * extent * 2 + extent * cols * 2) + slots * rows * cols * 18
     return pl.pallas_call(
-        coupling_kernel,
+        functools.partial(coupling_kernel, group),
         grid_spec=grid_spec,
         out_shape=[
             jax.ShapeDtypeStruct(own.shape, jnp.float32),
@@ -84,7 +97,7 @@
         global_slot.reshape(-1),
         flipped.astype(jnp.int32).reshape(-1),
         fock.reshape(-1),
-        every_amp,
+        *([every_amp] * group),
         s_ip,
         s_qj,
         own,

time: 162 us -> 153 us (0.944)
  Pallas kernels: 26.3 us -> 17 us
    pallas_call x1, Pallas kernels: 26.3 us -> 17 us  [couple_and_update(): pl.pallas_call(functools.partial(coupling_kernel, group), grid_spec=grid_...]
  transfers between devices with their start and end apart: 1 -> 1, of which waited for: 1 -> 1; matrix products, arithmetic and copies ran while one was open for 33% -> 35% of each run, Pallas kernels for 0% -> 0%
where the time goes in v3:
time: 153 us; the launch traced here: 152 us
  waiting for transfers between devices  66.5 us (43%)
  local copies, waits for them, and re-layouts  30.3 us (20%)
  matrix products  22.8 us (15%)
  Pallas kernels  17 us (11%)
  between operations  14.3 us (9%)
    all_gather x1, waiting for transfers between devices, shards(): every_amp = lax.all_gather(amplitudes, 'orb', axis=0, tiled=True)  65.8 us
    pallas_call x1, Pallas kernels, couple_and_update(): pl.pallas_call(functools.partial(coupling_kernel, group), grid_spec=grid_...  17 us
    gather x2, local copies, waits for them, and re-layouts, shards(): pao_energy[dom_j][:, None, :]  6.87 us
    gather x2, local copies, waits for them, and re-layouts, shards(): pao_energy[rows_dom][:, :, None] + pao_energy[dom_j][:, None, :]  6.87 us
    dot_general x1, matrix products, shards(): jnp.einsum('brk,bcpk->bcrp', rs, oh_p, preferred_element_type=jnp.float32)  5.48 us
    gather x1, local copies, waits for them, and re-layouts, shards(): pao_energy = jnp.diagonal(pao_fock).astype(jnp.float32)  4.82 us
    dot_general x1, matrix products, shards(): jnp.einsum('bcqk,bkj->bcqj', oh_q, col_s, preferred_element_type=jnp.floa...  4.58 us
  transfers between devices with their start and end apart: 1, of which 1 were waited for; matrix products, arithmetic and copies ran while one was open for 35% of the time, Pallas kernels for 0%

profile of v3, /device:TPU:0, one launch (start us, length us, event | category | flops | bytes accessed | tf_op | source)
XLA Modules:
  0.0 152.3 jit_solution(14214353327164489796)
XLA Ops:
  7.2 0.0 copy-start
  7.2 0.0 copy-start.2
  7.2 0.0 copy-start.3
  7.2 0.0 copy-start.7
  7.2 0.0 copy-start.5
  7.2 0.0 all-gather.2.cloned.1.call-start
  7.3 0.7 all-gather.2.cloned.1.call-update
  8.0 1.3 gather_fusion.6
  9.3 1.3 gather_fusion.3
  10.6 1.3 gather_fusion.8
  11.9 0.0 copy-done.3
  11.9 0.6 gather_fusion.4
  12.5 0.0 copy-done.2
  12.5 0.6 gather_fusion.9
  13.2 0.6 gather_fusion.7
  13.7 0.0 copy-done.7
  13.8 0.6 reshape.98.fock_ref
  14.4 0.0 copy-done.5
  14.4 4.8 %gather_fusion.10 = bf16[512]{0:T(512)(128)(2,1)S(1)} fusion(bf16[512,512]{1,0:T(8,128)(2,1)S(1)} %copy-done.5, s32[512]{0:T(512)S(1)} %bitcast.76), kind=kCustom, calls=%fused_computation.10 | custom fusion | bytes 6144 | tf_op jit(solution)/shard_map/jit(diagonal)/cond/branch_0_fun/gather | solution.py:182
  19.2 6.9 %gather_fusion.12 = f32[1024]{0:T(1024)S(1)} fusion(f32[512]{0:T(512)S(1)} %convert_element_type.65, s32[1024]{0:T(1024)S(1)} %broadcast_clamp_fusion), kind=kCustom, calls=%fused_computation.12 | custom fusion | bytes 12288 | tf_op jit(solution)/shard_map/gather | solution.py:184
  26.1 0.0 copy-start.8
  26.2 0.0 copy-start.9
  26.2 0.0 copy-start.1
  26.2 6.9 %gather_fusion.11 = f32[1024]{0:T(1024)S(1)} fusion(f32[512]{0:T(512)S(1)} %convert_element_type.65, s32[1024]{0:T(1024)S(1)} %broadcast_clamp_fusion.1), kind=kCustom, calls=%fused_computation.11 | custom fusion | bytes 12288 | tf_op jit(solution)/shard_map/gather | solution.py:184
  33.1 0.0 copy-done.8
  33.1 0.0 copy-done.9
  33.1 0.1 reshape.107
  33.2 0.0 copy-done.1
  33.2 0.0 copy-start.6
  33.2 0.8 gather_fusion.1
  33.9 0.6 reshape.95.slot_ref
  34.6 0.1 reshape.101
  34.6 0.8 gather_fusion
  35.4 0.1 reshape.104
  35.5 0.1 reshape.110
  35.6 0.0 copy-done.6
  35.6 0.1 reshape.115
  35.7 0.1 reshape.137
  35.8 0.6 reshape.100.flip_ref
  36.4 0.6 gather_fusion.2
  37.0 0.6 gather_fusion.5
  37.6 0.0 copy-done
  37.6 1.7 %fusion.19.clone.5 = bf16[4,256,512,1]{2,1,3,0:T(8,128)(2,1)} fusion(s32[4,256]{1,0:T(4,128)S(1)} %gather_fusion.7, bf16[512,512]{1,0:T(8,128)(2,1)S(1)} %copy-done), kind=kOutput, calls=%fused_computation.37.clone.clone.clone.2 | convolution fusion | flops 537919488 | bytes 1576960 | tf_op jit(solution)/shard_map/kc,bjc->bkj/dot_general | solution.py:161
  39.4 1.1 fusion.23
  40.5 1.9 %fusion.24 = bf16[4,256,256]{2,1,0:T(8,128)(2,1)} fusion(s32[4,256]{1,0:T(4,128)S(1)} %gather_fusion.7, bf16[512,512]{1,0:T(8,128)(2,1)S(1)} %copy-done.5), kind=kOutput, calls=%fused_computation.45 | convolution fusion | flops 807141376 | bytes 1052672 | tf_op jit(solution)/shard_map/bjk,bak->bja/dot_general | solution.py:160
  42.4 1.9 %fusion.21 = bf16[4,256,256]{2,1,0:T(8,128)(2,1)} fusion(s32[4,256]{1,0:T(4,128)S(1)} %gather_fusion.4, bf16[512,512]{1,0:T(8,128)(2,1)S(1)} %copy-done.5), kind=kOutput, calls=%fused_computation.42 | convolution fusion | flops 807141376 | bytes 1052672 | tf_op jit(solution)/shard_map/brk,bak->bra/dot_general | solution.py:156
  44.3 0.0 copy-start.4
  44.3 1.3 add_subtract_fusion.refs_7_
  45.6 0.8 fusion.14
  46.4 0.0 copy-start.10
  46.4 1.0 copy-done.10
  47.3 0.0 copy-done.4
  47.3 0.8 convolution_convert_fusion
  48.1 1.8 %convolution_add_fusion.1 = f32[4,256,256]{2,1,0:T(8,128)S(1)} fusion(bf16[4,256,256]{2,1,0:T(8,128)(2,1)S(1)} %fusion.23, bf16[4,256,256]{2,1,0:T(8,128)(2,1)} %fusion.21, bf16[4,256,256]{2,1,0:T(8,128)(2,1)S(1)} %copy-done.4, f32[1,4,256,256]{3,2,1,0:T(8,128)} %param.11), kind=kOutput, calls=%fused_computation.41 | convolution fusion | flops 268959744 | bytes 3670016 | tf_op jit(solution)/shard_map/brd,bdj->brj/dot_general | solution.py:176
  50.0 1.3 convolution_add_fusion
  51.3 0.0 copy-start.12
  51.3 1.3 fusion.20.refs_6_
  52.6 0.0 copy-done.12
  52.6 0.0 copy-start.11
  52.6 4.6 %fusion.4.refs_5_ = bf16[4,8,256,256]{3,2,1,0:T(8,128)(2,1)} fusion(s32[4,8,256]{2,1,0:T(8,128)S(1)} %bitcast.78, bf16[4,256,512,1]{2,1,3,0:T(8,128)(2,1)S(1)} %copy-done.12), kind=kOutput, calls=%fused_computation.20 | convolution fusion | flops 2153775104 | bytes 5275648 | tf_op jit(solution)/shard_map/bcqk,bkj->bcqj/dot_general | solution.py:165
  57.2 0.0 copy-done.11
  57.2 5.5 %convert_bitcast_fusion.refs_4_ = bf16[4,8,256,256]{3,2,1,0:T(8,128)(2,1)} fusion(s32[4,8,256]{2,1,0:T(8,128)S(1)} %bitcast.77, bf16[4,256,512]{2,1,0:T(8,128)(2,1)S(1)} %copy-done.11), kind=kOutput, calls=%fused_computation.19 | convolution fusion | flops 2153775104 | bytes 5275648 | tf_op jit(solution)/shard_map/brk,bcpk->bcrp/dot_general | solution.py:164
  62.7 65.8 %all-gather.2.cloned.1.call-done.refs_0_.refs_1_.refs_2_.refs_3_ = bf16[128,256,256]{2,1,0:T(8,128)(2,1)} async-done(((bf16[4,256,256]{2,1,0:T(8,128)(2,1)}), bf16[128,256,256]{2,1,0:T(8,128)(2,1)}) %all-gather.2.cloned.1.call-update) | async-done | bytes 16777232 | tf_op jit(solution)/shard_map/all_gather | solution.py:130
  128.5 17.0 %shard_map.122 = (f32[4,256,256]{2,1,0:T(8,128)}, bf16[4,256,256]{2,1,0:T(8,128)(2,1)}) custom-call(s32[32]{0:T(128)} %reshape.95.slot_ref, s32[32]{0:T(128)} %reshape.100.flip_ref, f32[32]{0:T(128)} %reshape.98.fock_ref, bf16[128,256,256]{2,1,0:T(8,128)(2,1)} %all-gather.2.cloned.1.call-done.refs_0_.refs_1_.refs_2_.refs_3_, ...), custom_call_target="tpu_custom_call" | custom-call | flops 2147483648 | bytes 17301504 | tf_op jit(solution)/shard_map/pallas_call | solution.py:87
  (23 shorter events, 0.1 us)
Async XLA Ops:
  7.2 30.5 %copy-start = (bf16[512,512]{1,0:T(8,128)(2,1)S(1)}, bf16[512,512]{1,0:T(8,128)(2,1)}, u32[]{:S(2)}) copy-start(bf16[512,512]{1,0:T(8,128)(2,1)} %param.15) | copy-start | bytes 1572868
  7.2 5.4 %copy-start.2 = (f32[64]{0:T(128)S(1)}, f32[64]{0:T(128)}, u32[]{:S(2)}) copy-start(f32[64]{0:T(128)} %param.17) | copy-start | bytes 772
  7.2 4.7 %copy-start.3 = (s32[64,256]{1,0:T(8,128)S(1)}, s32[64,256]{1,0:T(8,128)}, u32[]{:S(2)}) copy-start(s32[64,256]{1,0:T(8,128)} %param.14) | copy-start | bytes 196612
  7.2 6.5 %copy-start.7 = (f32[4,8]{1,0:T(4,128)S(1)}, f32[4,8]{1,0:T(4,128)}, u32[]{:S(2)}) copy-start(f32[4,8]{1,0:T(4,128)} %param.21) | copy-start | bytes 388
  7.2 7.1 %copy-start.5 = (bf16[512,512]{1,0:T(8,128)(2,1)S(1)}, bf16[512,512]{1,0:T(8,128)(2,1)}, u32[]{:S(2)}) copy-start(bf16[512,512]{1,0:T(8,128)(2,1)} %param.16) | copy-start | bytes 1572868
  7.2 121.3 %all-gather.2.cloned.1.call-start = ((), (), s32[]{:S(2)}) async-start(), calls=%async_computation | async-start | bytes 17301504 | tf_op jit(solution)/shard_map/all_gather | solution.py:130
  26.1 6.9 %copy-start.8 = (s32[4,8]{1,0:T(4,128)S(1)}, s32[4,8]{1,0:T(4,128)}, u32[]{:S(2)}) copy-start(s32[4,8]{1,0:T(4,128)} %param.19) | copy-start | bytes 388
  26.2 6.9 %copy-start.9 = (s32[4,8]{1,0:T(4,128)S(1)}, s32[4,8]{1,0:T(4,128)}, u32[]{:S(2)}) copy-start(s32[4,8]{1,0:T(4,128)} %param.18) | copy-start | bytes 388
  26.2 7.0 %copy-start.1 = (s32[128,2]{0,1:T(2,128)S(1)}, s32[128,2]{0,1:T(2,128)}, u32[]{:S(2)}) copy-start(s32[128,2]{0,1:T(2,128)} %param.13) | copy-start | bytes 3076
  33.2 2.4 %copy-start.6 = (s32[4,8]{1,0:T(4,128)S(1)}, s32[4,8]{1,0:T(4,128)}, u32[]{:S(2)}) copy-start(s32[4,8]{1,0:T(4,128)} %param.20) | copy-start | bytes 388
  44.3 3.0 %copy-start.4 = (bf16[4,256,256]{2,1,0:T(8,128)(2,1)S(1)}, bf16[4,256,256]{2,1,0:T(8,128)(2,1)}, u32[]{:S(2)}) copy-start(bf16[4,256,256]{2,1,0:T(8,128)(2,1)} %refs_8_) | copy-start | bytes 1572868
  46.4 1.0 copy-start.10
  51.3 1.3 copy-start.12
  52.6 4.6 %copy-start.11 = (bf16[4,256,512]{2,1,0:T(8,128)(2,1)S(1)}, bf16[4,256,512]{2,1,0:T(8,128)(2,1)}, u32[]{:S(2)}) copy-start(bf16[4,256,512]{2,1,0:T(8,128)(2,1)} %copy-done.10) | copy-start | bytes 3145732
Sparse Core Ops, SparseCore 0:
  10.9 117.5 all-gather.1

commit v4 on v3

--- a/solution.py
+++ b/solution.py
@@ -31,20 +31,10 @@
     total = res_ref[...]
     for k in range(group):
         at = (b * steps + step) * group + k
-
-        @pl.when(flip_ref[at] == 1)
-        def _():
-            reach[...] = lax.dot_general(
-                sip_ref[k], blk_refs[k][...], (((1,), (1,)), ((), ())), preferred_element_type=jnp.float32
-            ).astype(jnp.bfloat16)
-
-        @pl.when(flip_ref[at] != 1)
-        def _():
-            reach[...] = jnp.dot(sip_ref[k], blk_refs[k][...], preferred_element_type=jnp.float32).astype(
-                jnp.bfloat16
-            )
-
-        total = total - fock_ref[at] * jnp.dot(reach[...], sqj_ref[k], preferred_element_type=jnp.float32)
+        block = blk_refs[k][...]
+        block = jnp.where(flip_ref[at] == 1, block.T, block)
+        reach = jnp.dot(sip_ref[k], block, preferred_element_type=jnp.float32).astype(jnp.bfloat16)
+        total = total - fock_ref[at] * jnp.dot(reach, sqj_ref[k], preferred_element_type=jnp.float32)
     res_ref[...] = total
 
     @pl.when(step == steps - 1)
@@ -52,7 +42,7 @@
         upd_ref[...] = (amp_ref[...].astype(jnp.float32) - total / den_ref[...]).astype(jnp.bfloat16)
 
 
-def couple_and_update(every_amp, global_slot, flipped, fock, s_ip, s_qj, own, denom, amp_rows, group=4):
+def couple_and_update(every_amp, global_slot, flipped, fock, s_ip, s_qj, own, denom, amp_rows, group=8):
     slots, couplings = global_slot.shape
     group = group if couplings % group == 0 else 1
     steps = couplings // group

time: 153 us -> 145 us (0.948)
  Pallas kernels: 17 us -> 8.96 us
    pallas_call x1, Pallas kernels: 17 us -> 8.96 us  [couple_and_update(): pl.pallas_call(functools.partial(coupling_kernel, group), grid_spec=grid_...]
  transfers between devices with their start and end apart: 1 -> 1, of which waited for: 1 -> 1; matrix products, arithmetic and copies ran while one was open for 35% -> 37% of each run, Pallas kernels for 0% -> 0%
where the time goes in v4:
time: 145 us; the launch traced here: 144 us
  waiting for transfers between devices  66.5 us (46%)
  local copies, waits for them, and re-layouts  30.3 us (21%)
  matrix products  22.8 us (16%)
  between operations  14.4 us (10%)
  Pallas kernels  8.96 us (6%)
    all_gather x1, waiting for transfers between devices, shards(): every_amp = lax.all_gather(amplitudes, 'orb', axis=0, tiled=True)  65.8 us
    pallas_call x1, Pallas kernels, couple_and_update(): pl.pallas_call(functools.partial(coupling_kernel, group), grid_spec=grid_...  8.96 us
    gather x2, local copies, waits for them, and re-layouts, shards(): pao_energy[dom_j][:, None, :]  6.87 us
    gather x2, local copies, waits for them, and re-layouts, shards(): pao_energy[rows_dom][:, :, None] + pao_energy[dom_j][:, None, :]  6.87 us
    dot_general x1, matrix products, shards(): jnp.einsum('brk,bcpk->bcrp', rs, oh_p, preferred_element_type=jnp.float32)  5.48 us
    gather x1, local copies, waits for them, and re-layouts, shards(): pao_energy = jnp.diagonal(pao_fock).astype(jnp.float32)  4.82 us
    dot_general x1, matrix products, shards(): jnp.einsum('bcqk,bkj->bcqj', oh_q, col_s, preferred_element_type=jnp.floa...  4.58 us
  transfers between devices with their start and end apart: 1, of which 1 were waited for; matrix products, arithmetic and copies ran while one was open for 37% of the time, Pallas kernels for 0%

profile of v4, /device:TPU:0, one launch (start us, length us, event | category | flops | bytes accessed | tf_op | source)
XLA Modules:
  0.0 144.3 jit_solution(2170109521533566098)
XLA Ops:
  7.2 0.0 copy-start
  7.2 0.0 copy-start.2
  7.2 0.0 copy-start.3
  7.2 0.0 copy-start.7
  7.2 0.0 copy-start.5
  7.2 0.0 all-gather.2.cloned.1.call-start
  7.3 0.7 all-gather.2.cloned.1.call-update
  8.0 1.3 gather_fusion.6
  9.3 1.3 gather_fusion.3
  10.6 1.3 gather_fusion.8
  11.9 0.0 copy-done.3
  11.9 0.6 gather_fusion.4
  12.5 0.0 copy-done.2
  12.5 0.6 gather_fusion.9
  13.2 0.6 gather_fusion.7
  13.7 0.0 copy-done.7
  13.8 0.6 reshape.98.fock_ref
  14.4 0.0 copy-done.5
  14.4 4.8 %gather_fusion.10 = bf16[512]{0:T(512)(128)(2,1)S(1)} fusion(bf16[512,512]{1,0:T(8,128)(2,1)S(1)} %copy-done.5, s32[512]{0:T(512)S(1)} %bitcast.76), kind=kCustom, calls=%fused_computation.10 | custom fusion | bytes 6144 | tf_op jit(solution)/shard_map/jit(diagonal)/cond/branch_0_fun/gather | solution.py:172
  19.2 6.9 %gather_fusion.12 = f32[1024]{0:T(1024)S(1)} fusion(f32[512]{0:T(512)S(1)} %convert_element_type.65, s32[1024]{0:T(1024)S(1)} %broadcast_clamp_fusion), kind=kCustom, calls=%fused_computation.12 | custom fusion | bytes 12288 | tf_op jit(solution)/shard_map/gather | solution.py:174
  26.1 0.0 copy-start.8
  26.2 0.0 copy-start.9
  26.2 0.0 copy-start.1
  26.2 6.9 %gather_fusion.11 = f32[1024]{0:T(1024)S(1)} fusion(f32[512]{0:T(512)S(1)} %convert_element_type.65, s32[1024]{0:T(1024)S(1)} %broadcast_clamp_fusion.1), kind=kCustom, calls=%fused_computation.11 | custom fusion | bytes 12288 | tf_op jit(solution)/shard_map/gather | solution.py:174
  33.1 0.0 copy-done.8
  33.1 0.0 copy-done.9
  33.1 0.1 reshape.107
  33.2 0.0 copy-done.1
  33.2 0.0 copy-start.6
  33.2 0.8 gather_fusion.1
  33.9 0.6 reshape.95.slot_ref
  34.6 0.1 reshape.101
  34.6 0.8 gather_fusion
  35.4 0.1 reshape.104
  35.5 0.1 reshape.110
  35.6 0.0 copy-done.6
  35.6 0.1 reshape.115
  35.7 0.1 reshape.137
  35.8 0.6 reshape.100.flip_ref
  36.4 0.6 gather_fusion.2
  37.0 0.6 gather_fusion.5
  37.6 0.0 copy-done
  37.6 1.7 %fusion.19.clone.5 = bf16[4,256,512,1]{2,1,3,0:T(8,128)(2,1)} fusion(s32[4,256]{1,0:T(4,128)S(1)} %gather_fusion.7, bf16[512,512]{1,0:T(8,128)(2,1)S(1)} %copy-done), kind=kOutput, calls=%fused_computation.37.clone.clone.clone.2 | convolution fusion | flops 537919488 | bytes 1576960 | tf_op jit(solution)/shard_map/kc,bjc->bkj/dot_general | solution.py:151
  39.4 1.1 fusion.23
  40.5 1.9 %fusion.24 = bf16[4,256,256]{2,1,0:T(8,128)(2,1)} fusion(s32[4,256]{1,0:T(4,128)S(1)} %gather_fusion.7, bf16[512,512]{1,0:T(8,128)(2,1)S(1)} %copy-done.5), kind=kOutput, calls=%fused_computation.45 | convolution fusion | flops 807141376 | bytes 1052672 | tf_op jit(solution)/shard_map/bjk,bak->bja/dot_general | solution.py:150
  42.4 1.9 %fusion.21 = bf16[4,256,256]{2,1,0:T(8,128)(2,1)} fusion(s32[4,256]{1,0:T(4,128)S(1)} %gather_fusion.4, bf16[512,512]{1,0:T(8,128)(2,1)S(1)} %copy-done.5), kind=kOutput, calls=%fused_computation.42 | convolution fusion | flops 807141376 | bytes 1052672 | tf_op jit(solution)/shard_map/brk,bak->bra/dot_general | solution.py:146
  44.3 0.0 copy-start.4
  44.3 1.3 add_subtract_fusion.refs_11_
  45.6 0.8 fusion.14
  46.4 0.0 copy-start.10
  46.4 1.0 copy-done.10
  47.3 0.0 copy-done.4
  47.3 0.8 convolution_convert_fusion
  48.1 1.8 %convolution_add_fusion.1 = f32[4,256,256]{2,1,0:T(8,128)S(1)} fusion(bf16[4,256,256]{2,1,0:T(8,128)(2,1)S(1)} %fusion.23, bf16[4,256,256]{2,1,0:T(8,128)(2,1)} %fusion.21, bf16[4,256,256]{2,1,0:T(8,128)(2,1)S(1)} %copy-done.4, f32[1,4,256,256]{3,2,1,0:T(8,128)} %param.11), kind=kOutput, calls=%fused_computation.41 | convolution fusion | flops 268959744 | bytes 3670016 | tf_op jit(solution)/shard_map/brd,bdj->brj/dot_general | solution.py:166
  50.0 1.3 convolution_add_fusion
  51.3 0.0 copy-start.12
  51.3 1.3 fusion.20.refs_10_
  52.6 0.0 copy-done.12
  52.6 0.0 copy-start.11
  52.6 4.6 %fusion.4.refs_9_ = bf16[4,8,256,256]{3,2,1,0:T(8,128)(2,1)} fusion(s32[4,8,256]{2,1,0:T(8,128)S(1)} %bitcast.78, bf16[4,256,512,1]{2,1,3,0:T(8,128)(2,1)S(1)} %copy-done.12), kind=kOutput, calls=%fused_computation.20 | convolution fusion | flops 2153775104 | bytes 5275648 | tf_op jit(solution)/shard_map/bcqk,bkj->bcqj/dot_general | solution.py:155
  57.2 0.0 copy-done.11
  57.2 5.5 %convert_bitcast_fusion.refs_8_ = bf16[4,8,256,256]{3,2,1,0:T(8,128)(2,1)} fusion(s32[4,8,256]{2,1,0:T(8,128)S(1)} %bitcast.77, bf16[4,256,512]{2,1,0:T(8,128)(2,1)S(1)} %copy-done.11), kind=kOutput, calls=%fused_computation.19 | convolution fusion | flops 2153775104 | bytes 5275648 | tf_op jit(solution)/shard_map/brk,bcpk->bcrp/dot_general | solution.py:154
  62.7 65.8 %all-gather.2.cloned.1.call-done.refs_0_.refs_1_.refs_2_.refs_3_.refs_4_.refs_5_.refs_6_.refs_7_ = bf16[128,256,256]{2,1,0:T(8,128)(2,1)} async-done(((bf16[4,256,256]{2,1,0:T(8,128)(2,1)}), bf16[128,256,256]{2,1,0:T(8,128)(2,1)}) %all-gather.2.cloned.1.call-update) | async-done | bytes 16777232 | tf_op jit(solution)/shard_map/all_gather | solution.py:120
  128.5 9.0 %shard_map.122 = (f32[4,256,256]{2,1,0:T(8,128)}, bf16[4,256,256]{2,1,0:T(8,128)(2,1)}) custom-call(s32[32]{0:T(128)} %reshape.95.slot_ref, s32[32]{0:T(128)} %reshape.100.flip_ref, f32[32]{0:T(128)} %reshape.98.fock_ref, bf16[128,256,256]{2,1,0:T(8,128)(2,1)} %all-gather.2.cloned.1.call-done.refs_0_.refs_1_.refs_2_.refs_3_.refs_4_.refs_5_.refs_6_.refs_7_, ...), custom_call_target="tpu_custom_call" | custom-call | flops 2147483648 | bytes 17301504 | tf_op jit(solution)/shard_map/pallas_call | solution.py:77
  (23 shorter events, 0.1 us)
Async XLA Ops:
  7.2 30.5 %copy-start = (bf16[512,512]{1,0:T(8,128)(2,1)S(1)}, bf16[512,512]{1,0:T(8,128)(2,1)}, u32[]{:S(2)}) copy-start(bf16[512,512]{1,0:T(8,128)(2,1)} %param.15) | copy-start | bytes 1572868
  7.2 5.4 %copy-start.2 = (f32[64]{0:T(128)S(1)}, f32[64]{0:T(128)}, u32[]{:S(2)}) copy-start(f32[64]{0:T(128)} %param.17) | copy-start | bytes 772
  7.2 4.7 %copy-start.3 = (s32[64,256]{1,0:T(8,128)S(1)}, s32[64,256]{1,0:T(8,128)}, u32[]{:S(2)}) copy-start(s32[64,256]{1,0:T(8,128)} %param.14) | copy-start | bytes 196612
  7.2 6.5 %copy-start.7 = (f32[4,8]{1,0:T(4,128)S(1)}, f32[4,8]{1,0:T(4,128)}, u32[]{:S(2)}) copy-start(f32[4,8]{1,0:T(4,128)} %param.21) | copy-start | bytes 388
  7.2 7.1 %copy-start.5 = (bf16[512,512]{1,0:T(8,128)(2,1)S(1)}, bf16[512,512]{1,0:T(8,128)(2,1)}, u32[]{:S(2)}) copy-start(bf16[512,512]{1,0:T(8,128)(2,1)} %param.16) | copy-start | bytes 1572868
  7.2 121.3 %all-gather.2.cloned.1.call-start = ((), (), s32[]{:S(2)}) async-start(), calls=%async_computation | async-start | bytes 17301504 | tf_op jit(solution)/shard_map/all_gather | solution.py:120
  26.1 6.9 %copy-start.8 = (s32[4,8]{1,0:T(4,128)S(1)}, s32[4,8]{1,0:T(4,128)}, u32[]{:S(2)}) copy-start(s32[4,8]{1,0:T(4,128)} %param.19) | copy-start | bytes 388
  26.2 6.9 %copy-start.9 = (s32[4,8]{1,0:T(4,128)S(1)}, s32[4,8]{1,0:T(4,128)}, u32[]{:S(2)}) copy-start(s32[4,8]{1,0:T(4,128)} %param.18) | copy-start | bytes 388
  26.2 7.0 %copy-start.1 = (s32[128,2]{0,1:T(2,128)S(1)}, s32[128,2]{0,1:T(2,128)}, u32[]{:S(2)}) copy-start(s32[128,2]{0,1:T(2,128)} %param.13) | copy-start | bytes 3076
  33.2 2.4 %copy-start.6 = (s32[4,8]{1,0:T(4,128)S(1)}, s32[4,8]{1,0:T(4,128)}, u32[]{:S(2)}) copy-start(s32[4,8]{1,0:T(4,128)} %param.20) | copy-start | bytes 388
  44.3 3.0 %copy-start.4 = (bf16[4,256,256]{2,1,0:T(8,128)(2,1)S(1)}, bf16[4,256,256]{2,1,0:T(8,128)(2,1)}, u32[]{:S(2)}) copy-start(bf16[4,256,256]{2,1,0:T(8,128)(2,1)} %refs_12_) | copy-start | bytes 1572868
  46.4 1.0 copy-start.10
  51.3 1.3 copy-start.12
  52.6 4.6 %copy-start.11 = (bf16[4,256,512]{2,1,0:T(8,128)(2,1)S(1)}, bf16[4,256,512]{2,1,0:T(8,128)(2,1)}, u32[]{:S(2)}) copy-start(bf16[4,256,512]{2,1,0:T(8,128)(2,1)} %copy-done.10) | copy-start | bytes 3145732
Sparse Core Ops, SparseCore 0:
  10.9 117.5 all-gather.1

commit v5 on v4

--- a/solution.py
+++ b/solution.py
@@ -18,9 +18,10 @@
     ).astype(jnp.bfloat16)
 
 
-def coupling_kernel(group, slot_ref, flip_ref, fock_ref, *refs):
+def coupling_kernel(group, slot_ref, flip_ref, fock_ref, esum_ref, *refs):
     blk_refs = refs[:group]
-    sip_ref, sqj_ref, own_ref, den_ref, amp_ref, res_ref, upd_ref, reach = refs[group:]
+    both_ref, own_ref, erow_ref, ecol_ref, amp_ref, res_ref, upd_ref = refs[group:]
+    rows = own_ref.shape[0]
     b, step = pl.program_id(0), pl.program_id(1)
     steps = pl.num_programs(1)
 
@@ -33,16 +34,19 @@
         at = (b * steps + step) * group + k
         block = blk_refs[k][...]
         block = jnp.where(flip_ref[at] == 1, block.T, block)
-        reach = jnp.dot(sip_ref[k], block, preferred_element_type=jnp.float32).astype(jnp.bfloat16)
-        total = total - fock_ref[at] * jnp.dot(reach, sqj_ref[k], preferred_element_type=jnp.float32)
+        reach = jnp.dot(both_ref[k, :rows], block, preferred_element_type=jnp.float32).astype(jnp.bfloat16)
+        total = total - fock_ref[at] * jnp.dot(reach, both_ref[k, rows:], preferred_element_type=jnp.float32)
     res_ref[...] = total
 
     @pl.when(step == steps - 1)
     def _():
-        upd_ref[...] = (amp_ref[...].astype(jnp.float32) - total / den_ref[...]).astype(jnp.bfloat16)
-
-
-def couple_and_update(every_amp, global_slot, flipped, fock, s_ip, s_qj, own, denom, amp_rows, group=8):
+        denom = erow_ref[...] + ecol_ref[...] - esum_ref[b]
+        upd_ref[...] = (amp_ref[...].astype(jnp.float32) - total / denom).astype(jnp.bfloat16)
+
+
+def couple_and_update(
+    every_amp, global_slot, flipped, fock, s_ip, s_qj, own, e_rows, e_cols, energy_sum, amp_rows, group=8
+):
     slots, couplings = global_slot.shape
     group = group if couplings % group == 0 else 1
     steps = couplings // group
@@ -51,26 +55,25 @@
 
     def block_spec(k):
         return pl.BlockSpec(
-            (None, extent, extent), lambda b, t, gs, fl, fe: (gs[(b * steps + t) * group + k], 0, 0)
+            (None, extent, extent), lambda b, t, gs, fl, fe, es: (gs[(b * steps + t) * group + k], 0, 0)
         )
 
-    per_slot = lambda b, t, gs, fl, fe: (b, 0, 0)
+    per_slot = lambda b, t, gs, fl, fe, es: (b, 0, 0)
     grid_spec = pltpu.PrefetchScalarGridSpec(
-        num_scalar_prefetch=3,
+        num_scalar_prefetch=4,
         grid=(slots, steps),
         in_specs=[block_spec(k) for k in range(group)]
         + [
-            pl.BlockSpec((None, group, rows, extent), lambda b, t, gs, fl, fe: (b, t, 0, 0)),
-            pl.BlockSpec((None, group, extent, cols), lambda b, t, gs, fl, fe: (b, t, 0, 0)),
-            pl.BlockSpec((None, rows, cols), per_slot),
-            pl.BlockSpec((None, rows, cols), per_slot),
+            pl.BlockSpec((None, group, rows + extent, extent), lambda b, t, gs, fl, fe, es: (b, t, 0, 0)),
+            pl.BlockSpec((None, rows, cols), per_slot),
+            pl.BlockSpec((None, rows, 1), per_slot),
+            pl.BlockSpec((None, 1, cols), per_slot),
             pl.BlockSpec((None, rows, cols), per_slot),
         ],
         out_specs=[
             pl.BlockSpec((None, rows, cols), per_slot),
             pl.BlockSpec((None, rows, cols), per_slot),
         ],
-        scratch_shapes=[pltpu.VMEM((rows, extent), jnp.bfloat16)],
     )
     flops = 4 * slots * couplings * rows * extent * extent
     moved = slots * couplings * (extent * extent * 2 + rows * extent * 2 + extent * cols * 2) + slots * rows * cols * 18
@@ -87,11 +90,12 @@
         global_slot.reshape(-1),
         flipped.astype(jnp.int32).reshape(-1),
         fock.reshape(-1),
+        energy_sum,
         *([every_amp] * group),
-        s_ip,
-        s_qj,
+        jnp.concatenate([s_ip, s_qj], axis=2),
         own,
-        denom,
+        e_rows[:, :, None],
+        e_cols[:, None, :],
         amp_rows,
     )
 
@@ -170,12 +174,19 @@
     )
 
     pao_energy = jnp.diagonal(pao_fock).astype(jnp.float32)
-    denom = (
-        pao_energy[rows_dom][:, :, None] + pao_energy[dom_j][:, None, :] - energy_sum[:, None, None]
-    )
     amp_rows = lax.dynamic_slice_in_dim(amplitudes, row_first, half_rows, 1)
     return couple_and_update(
-        every_amp, global_slot, flipped, coupling_fock_element, s_ip, s_qj, summed, denom, amp_rows
+        every_amp,
+        global_slot,
+        flipped,
+        coupling_fock_element,
+        s_ip,
+        s_qj,
+        summed,
+        pao_energy[rows_dom],
+        pao_energy[dom_j],
+        energy_sum,
+        amp_rows,
     )
 
 

time: 145 us -> 145 us (level)
  waiting for transfers between devices: 66.5 us -> 49.3 us
  local copies, waits for them, and re-layouts: 30.3 us -> 38.1 us
  other arithmetic: 1.37 us -> 8.63 us
  matrix products: 22.8 us -> 25 us
    all_gather x1, waiting for transfers between devices: 65.8 us -> 48.6 us  [shards(): every_amp = lax.all_gather(amplitudes, 'orb', axis=0, tiled=True)]
    concatenate x0 -> x1, other arithmetic: none -> 7.82 us  [couple_and_update(): jnp.concatenate([s_ip, s_qj], axis=2)]
    gather x4 -> x2, local copies, waits for them, and re-layouts: 13.7 us -> 18.2 us  [the longest x1 11.3 us: shards(): pao_energy[dom_j]]
  transfers between devices with their start and end apart: 1 -> 1, of which waited for: 1 -> 1; matrix products, arithmetic and copies ran while one was open for 37% -> 50% of each run, Pallas kernels for 0% -> 0%
where the time goes in v5:
time: 145 us; the launch traced here: 144 us
  waiting for transfers between devices  49.3 us (34%)
  local copies, waits for them, and re-layouts  38.1 us (26%)
  matrix products  25 us (17%)
  between operations  14.2 us (10%)
  Pallas kernels  8.84 us (6%)
  other arithmetic  8.63 us (6%)
    all_gather x1, waiting for transfers between devices, shards(): every_amp = lax.all_gather(amplitudes, 'orb', axis=0, tiled=True)  48.6 us
    gather x1, local copies, waits for them, and re-layouts, shards(): pao_energy[dom_j]  11.3 us
    pallas_call x1, Pallas kernels, couple_and_update(): pl.pallas_call(functools.partial(coupling_kernel, group), grid_spec=grid_...  8.84 us
    concatenate x1, other arithmetic, couple_and_update(): jnp.concatenate([s_ip, s_qj], axis=2)  7.82 us
    gather x1, local copies, waits for them, and re-layouts, shards(): pao_energy[rows_dom]  6.87 us
    dot_general x1, matrix products, shards(): jnp.einsum('brk,bcpk->bcrp', rs, oh_p, preferred_element_type=jnp.float32)  5.39 us
    gather x1, local copies, waits for them, and re-layouts, shards(): pao_energy = jnp.diagonal(pao_fock).astype(jnp.float32)  4.85 us
    dot_general x1, matrix products, shards(): jnp.einsum('bcqk,bkj->bcqj', oh_q, col_s, preferred_element_type=jnp.floa...  4.59 us
  transfers between devices with their start and end apart: 1, of which 1 were waited for; matrix products, arithmetic and copies ran while one was open for 50% of the time, Pallas kernels for 0%

profile of v5, /device:TPU:0, one launch (start us, length us, event | category | flops | bytes accessed | tf_op | source)
XLA Modules:
  0.0 144.2 jit_solution(757908599066477688)
XLA Ops:
  7.2 0.0 copy-start
  7.2 0.0 copy-start.1
  7.2 0.0 copy-start.2
  7.2 0.0 copy-start.5
  7.2 0.0 copy-start.4
  7.2 0.0 all-gather.2.cloned.1.call-start
  7.3 0.7 all-gather.2.cloned.1.call-update
  8.0 1.3 gather_fusion
  9.3 1.3 gather_fusion.2
  10.6 1.4 gather_fusion.7
  12.1 1.4 gather_fusion.9
  13.5 1.3 gather_fusion.1
  14.8 1.3 gather_fusion.3
  16.1 0.7 broadcast_or_fusion
  16.8 0.6 reshape.93.slot_ref
  17.4 0.1 reshape.133
  17.5 1.4 gather_fusion.5
  18.9 0.1 reshape.136
  19.0 0.1 reshape.127
  19.1 0.0 copy-done.1
  19.1 0.8 gather_fusion.4
  19.9 0.1 reshape.130
  19.9 0.0 copy-done.5
  20.0 0.1 reshape.157
  20.1 0.0 copy-done.2
  20.1 0.6 gather_fusion.8
  20.7 0.1 reshape.141
  20.8 0.6 gather_fusion.6
  21.4 0.7 reshape.98.flip_ref
  22.0 0.0 copy-done.4
  22.1 4.8 %gather_fusion.10 = bf16[512]{0:T(512)(128)(2,1)S(1)} fusion(bf16[512,512]{1,0:T(8,128)(2,1)S(1)} %copy-done.4, s32[512]{0:T(512)S(1)} %bitcast.77), kind=kCustom, calls=%fused_computation.10 | custom fusion | bytes 6144 | tf_op jit(solution)/shard_map/jit(diagonal)/cond/branch_0_fun/gather | solution.py:176
  26.9 0.0 copy-start.6
  26.9 6.9 %gather_fusion.11 = f32[1024]{0:T(1024)S(1)} fusion(f32[512]{0:T(512)S(1)} %convert_element_type.66, s32[1024]{0:T(1024)S(1)} %broadcast_clamp_fusion.1), kind=kCustom, calls=%fused_computation.11 | custom fusion | bytes 12288 | tf_op jit(solution)/shard_map/gather | solution.py:186
  33.8 1.2 broadcast_in_dim.17.refs_10_
  35.0 11.3 %gather_fusion.12 = f32[1024]{0:T(1024)} fusion(f32[512]{0:T(512)S(1)} %convert_element_type.66, s32[1024]{0:T(1024)S(1)} %broadcast_clamp_fusion), kind=kCustom, calls=%fused_computation.12 | custom fusion | bytes 12288 | tf_op jit(solution)/shard_map/gather | solution.py:187
  46.3 0.0 copy-done.6
  46.3 0.7 reshape.96.fock_ref
  47.0 0.0 copy-done
  47.0 0.0 copy-start.7
  47.0 1.7 %fusion.19.clone.5 = bf16[4,256,512,1]{2,1,3,0:T(8,128)(2,1)} fusion(s32[4,256]{1,0:T(4,128)S(1)} %gather_fusion.9, bf16[512,512]{1,0:T(8,128)(2,1)S(1)} %copy-done), kind=kOutput, calls=%fused_computation.38.clone.clone.clone.2 | convolution fusion | flops 537919488 | bytes 1576960 | tf_op jit(solution)/shard_map/kc,bjc->bkj/dot_general | solution.py:155
  48.7 1.1 fusion.23
  49.8 1.9 %fusion.21 = bf16[4,256,256]{2,1,0:T(8,128)(2,1)} fusion(s32[4,256]{1,0:T(4,128)S(1)} %gather_fusion.7, bf16[512,512]{1,0:T(8,128)(2,1)S(1)} %copy-done.4), kind=kOutput, calls=%fused_computation.43 | convolution fusion | flops 807141376 | bytes 1052672 | tf_op jit(solution)/shard_map/brk,bak->bra/dot_general | solution.py:150
  51.7 0.0 copy-start.3
  51.7 1.9 %fusion.24 = bf16[4,256,256]{2,1,0:T(8,128)(2,1)} fusion(s32[4,256]{1,0:T(4,128)S(1)} %gather_fusion.9, bf16[512,512]{1,0:T(8,128)(2,1)S(1)} %copy-done.4), kind=kOutput, calls=%fused_computation.46 | convolution fusion | flops 807141376 | bytes 1052672 | tf_op jit(solution)/shard_map/bjk,bak->bja/dot_general | solution.py:154
  53.7 1.8 %fusion.14 = bf16[4,256,512]{2,1,0:T(8,128)(2,1)} fusion(s32[4,256]{1,0:T(4,128)S(1)} %gather_fusion.7, bf16[512,512]{1,0:T(8,128)(2,1)S(1)} %copy-done), kind=kOutput, calls=%fused_computation.33 | convolution fusion | flops 537919488 | bytes 1576960 | tf_op jit(solution)/shard_map/...rk,kc->...rc/dot_general | solution.py:16
  55.5 0.0 copy-done.3
  55.5 2.0 %convolution_convert_fusion = bf16[4,256,256]{2,1,0:T(8,128)(2,1)S(1)} fusion(bf16[4,256,256]{2,1,0:T(8,128)(2,1)S(1)} %copy-done.3, bf16[4,256,512]{2,1,0:T(8,128)(2,1)} %fusion.14, s32[4,256]{1,0:T(4,128)S(1)} %gather_fusion.7), kind=kOutput, calls=%fused_computation.47 | convolution fusion | flops 403701760 | bytes 2101248 | tf_op jit(solution)/shard_map/bra,bad->brd/dot_general | solution.py:167
  57.5 1.8 %convolution_add_fusion.1 = f32[4,256,256]{2,1,0:T(8,128)S(1)} fusion(bf16[4,256,256]{2,1,0:T(8,128)(2,1)S(1)} %fusion.23, bf16[4,256,256]{2,1,0:T(8,128)(2,1)} %fusion.21, bf16[4,256,256]{2,1,0:T(8,128)(2,1)S(1)} %copy-done.3, f32[1,4,256,256]{3,2,1,0:T(8,128)} %param.11), kind=kOutput, calls=%fused_computation.42 | convolution fusion | flops 268959744 | bytes 3670016 | tf_op jit(solution)/shard_map/brd,bdj->brj/dot_general | solution.py:170
  59.3 0.0 copy-start.9
  59.3 1.4 convolution_add_fusion
  60.8 0.0 copy-done.7
  60.8 1.3 fusion.20.refs_9_
  62.1 0.0 copy-done.9
  62.1 0.0 copy-start.8
  62.1 4.6 %fusion.4 = bf16[4,8,256,256]{3,2,1,0:T(8,128)(2,1)} fusion(s32[4,8,256]{2,1,0:T(8,128)S(1)} %bitcast.78, bf16[4,256,512,1]{2,1,3,0:T(8,128)(2,1)S(1)} %copy-done.9), kind=kOutput, calls=%fused_computation.21 | convolution fusion | flops 2153775104 | bytes 5275648 | tf_op jit(solution)/shard_map/bcqk,bkj->bcqj/dot_general | solution.py:159
  66.7 0.0 copy-done.8
  66.7 5.4 %convert_bitcast_fusion = bf16[4,8,256,256]{3,2,1,0:T(8,128)(2,1)} fusion(s32[4,8,256]{2,1,0:T(8,128)S(1)} %bitcast.79, bf16[4,256,512]{2,1,0:T(8,128)(2,1)S(1)} %copy-done.8), kind=kOutput, calls=%fused_computation.20 | convolution fusion | flops 2153775104 | bytes 5275648 | tf_op jit(solution)/shard_map/brk,bcpk->bcrp/dot_general | solution.py:158
  72.1 7.8 %pad_maximum_fusion.refs_8_ = bf16[4,8,512,256]{3,2,1,0:T(8,128)(2,1)} fusion(bf16[4,8,256,256]{3,2,1,0:T(8,128)(2,1)} %fusion.4, bf16[4,8,256,256]{3,2,1,0:T(8,128)(2,1)} %convert_bitcast_fusion), kind=kLoop, calls=%fused_computation.17 | loop fusion | flops 16777216 | bytes 16777216 | tf_op jit(solution)/shard_map/concatenate | solution.py:95
  79.9 48.6 %all-gather.2.cloned.1.call-done.refs_0_.refs_1_.refs_2_.refs_3_.refs_4_.refs_5_.refs_6_.refs_7_ = bf16[128,256,256]{2,1,0:T(8,128)(2,1)} async-done(((bf16[4,256,256]{2,1,0:T(8,128)(2,1)}), bf16[128,256,256]{2,1,0:T(8,128)(2,1)}) %all-gather.2.cloned.1.call-update) | async-done | bytes 16777232 | tf_op jit(solution)/shard_map/all_gather | solution.py:124
  128.5 8.8 %shard_map.122 = (f32[4,256,256]{2,1,0:T(8,128)}, bf16[4,256,256]{2,1,0:T(8,128)(2,1)}) custom-call(s32[32]{0:T(128)} %reshape.93.slot_ref, s32[32]{0:T(128)} %reshape.98.flip_ref, f32[32]{0:T(128)} %reshape.96.fock_ref, f32[4]{0:T(128)} %copy-done.7, ...), custom_call_target="tpu_custom_call" | custom-call | flops 2147483648 | bytes 17301504 | tf_op jit(solution)/shard_map/pallas_call | solution.py:80
  (20 shorter events, 0.1 us)
Async XLA Ops:
  7.2 39.8 %copy-start = (bf16[512,512]{1,0:T(8,128)(2,1)S(1)}, bf16[512,512]{1,0:T(8,128)(2,1)}, u32[]{:S(2)}) copy-start(bf16[512,512]{1,0:T(8,128)(2,1)} %param.15) | copy-start | bytes 1572868
  7.2 11.9 %copy-start.1 = (s32[128,2]{0,1:T(2,128)S(1)}, s32[128,2]{0,1:T(2,128)}, u32[]{:S(2)}) copy-start(s32[128,2]{0,1:T(2,128)} %param.13) | copy-start | bytes 3076
  7.2 12.9 %copy-start.2 = (s32[64,256]{1,0:T(8,128)S(1)}, s32[64,256]{1,0:T(8,128)}, u32[]{:S(2)}) copy-start(s32[64,256]{1,0:T(8,128)} %param.14) | copy-start | bytes 196612
  7.2 12.7 %copy-start.5 = (s32[4,8]{1,0:T(4,128)S(1)}, s32[4,8]{1,0:T(4,128)}, u32[]{:S(2)}) copy-start(s32[4,8]{1,0:T(4,128)} %param.20) | copy-start | bytes 388
  7.2 14.8 %copy-start.4 = (bf16[512,512]{1,0:T(8,128)(2,1)S(1)}, bf16[512,512]{1,0:T(8,128)(2,1)}, u32[]{:S(2)}) copy-start(bf16[512,512]{1,0:T(8,128)(2,1)} %param.16) | copy-start | bytes 1572868
  7.2 121.3 %all-gather.2.cloned.1.call-start = ((), (), s32[]{:S(2)}) async-start(), calls=%async_computation | async-start | bytes 17301504 | tf_op jit(solution)/shard_map/all_gather | solution.py:124
  26.9 19.4 %copy-start.6 = (f32[4,8]{1,0:T(4,128)S(1)}, f32[4,8]{1,0:T(4,128)}, u32[]{:S(2)}) copy-start(f32[4,8]{1,0:T(4,128)} %param.21) | copy-start | bytes 388
  47.0 13.8 %copy-start.7 = (f32[4]{0:T(128)}, f32[4]{0:T(128)S(1)}, u32[]{:S(2)}) copy-start(f32[4]{0:T(128)S(1)} %add.109.esum_ref) | copy-start | bytes 52
  51.7 3.7 %copy-start.3 = (bf16[4,256,256]{2,1,0:T(8,128)(2,1)S(1)}, bf16[4,256,256]{2,1,0:T(8,128)(2,1)}, u32[]{:S(2)}) copy-start(bf16[4,256,256]{2,1,0:T(8,128)(2,1)} %refs_12_) | copy-start | bytes 1572868
  59.3 2.8 %copy-start.9 = (bf16[4,256,512,1]{2,1,3,0:T(8,128)(2,1)S(1)}, bf16[4,256,512,1]{2,1,3,0:T(8,128)(2,1)}, u32[]{:S(2)}) copy-start(bf16[4,256,512,1]{2,1,3,0:T(8,128)(2,1)} %fusion.19.clone.5) | copy-start | bytes 3145732
  62.1 4.6 %copy-start.8 = (bf16[4,256,512]{2,1,0:T(8,128)(2,1)S(1)}, bf16[4,256,512]{2,1,0:T(8,128)(2,1)}, u32[]{:S(2)}) copy-start(bf16[4,256,512]{2,1,0:T(8,128)(2,1)} %fusion.14) | copy-start | bytes 3145732
Sparse Core Ops, SparseCore 0:
  10.9 117.5 all-gather.1

commit v6 on v4

--- a/solution.py
+++ b/solution.py
@@ -18,9 +18,10 @@
     ).astype(jnp.bfloat16)
 
 
-def coupling_kernel(group, slot_ref, flip_ref, fock_ref, *refs):
+def coupling_kernel(group, slot_ref, last_ref, pick_ref, flip_ref, fock_ref, *refs):
     blk_refs = refs[:group]
-    sip_ref, sqj_ref, own_ref, den_ref, amp_ref, res_ref, upd_ref, reach = refs[group:]
+    tail_refs = refs[group:2 * group]
+    sip_ref, sqj_ref, own_ref, den_ref, amp_ref, res_ref, upd_ref, reach = refs[2 * group:]
     b, step = pl.program_id(0), pl.program_id(1)
     steps = pl.num_programs(1)
 
@@ -31,7 +32,7 @@
     total = res_ref[...]
     for k in range(group):
         at = (b * steps + step) * group + k
-        block = blk_refs[k][...]
+        block = jnp.where(pick_ref[at] == 1, tail_refs[k][...], blk_refs[k][...])
         block = jnp.where(flip_ref[at] == 1, block.T, block)
         reach = jnp.dot(sip_ref[k], block, preferred_element_type=jnp.float32).astype(jnp.bfloat16)
         total = total - fock_ref[at] * jnp.dot(reach, sqj_ref[k], preferred_element_type=jnp.float32)
@@ -42,26 +43,34 @@
         upd_ref[...] = (amp_ref[...].astype(jnp.float32) - total / den_ref[...]).astype(jnp.bfloat16)
 
 
-def couple_and_update(every_amp, global_slot, flipped, fock, s_ip, s_qj, own, denom, amp_rows, group=8):
-    slots, couplings = global_slot.shape
+def couple_and_update(
+    head_amp, tail_amp, head_slot, tail_slot, pick, flipped, fock, s_ip, s_qj, own, denom, amp_rows, group=8
+):
+    slots, couplings = head_slot.shape
     group = group if couplings % group == 0 else 1
     steps = couplings // group
     rows, cols = own.shape[1], own.shape[2]
-    extent = every_amp.shape[1]
+    extent = head_amp.shape[1]
 
     def block_spec(k):
         return pl.BlockSpec(
-            (None, extent, extent), lambda b, t, gs, fl, fe: (gs[(b * steps + t) * group + k], 0, 0)
+            (None, extent, extent), lambda b, t, gs, ls, pk, fl, fe: (gs[(b * steps + t) * group + k], 0, 0)
         )
 
-    per_slot = lambda b, t, gs, fl, fe: (b, 0, 0)
+    def tail_spec(k):
+        return pl.BlockSpec(
+            (None, extent, extent), lambda b, t, gs, ls, pk, fl, fe: (ls[(b * steps + t) * group + k], 0, 0)
+        )
+
+    per_slot = lambda b, t, gs, ls, pk, fl, fe: (b, 0, 0)
     grid_spec = pltpu.PrefetchScalarGridSpec(
-        num_scalar_prefetch=3,
+        num_scalar_prefetch=5,
         grid=(slots, steps),
         in_specs=[block_spec(k) for k in range(group)]
+        + [tail_spec(k) for k in range(group)]
         + [
-            pl.BlockSpec((None, group, rows, extent), lambda b, t, gs, fl, fe: (b, t, 0, 0)),
-            pl.BlockSpec((None, group, extent, cols), lambda b, t, gs, fl, fe: (b, t, 0, 0)),
+            pl.BlockSpec((None, group, rows, extent), lambda b, t, gs, ls, pk, fl, fe: (b, t, 0, 0)),
+            pl.BlockSpec((None, group, extent, cols), lambda b, t, gs, ls, pk, fl, fe: (b, t, 0, 0)),
             pl.BlockSpec((None, rows, cols), per_slot),
             pl.BlockSpec((None, rows, cols), per_slot),
             pl.BlockSpec((None, rows, cols), per_slot),
@@ -84,10 +93,13 @@
         compiler_params=pltpu.CompilerParams(dimension_semantics=("arbitrary", "arbitrary")),
         cost_estimate=pl.CostEstimate(flops=flops, bytes_accessed=moved, transcendentals=0),
     )(
-        global_slot.reshape(-1),
+        head_slot.reshape(-1),
+        tail_slot.reshape(-1),
+        pick.astype(jnp.int32).reshape(-1),
         flipped.astype(jnp.int32).reshape(-1),
         fock.reshape(-1),
-        *([every_amp] * group),
+        *([head_amp] * group),
+        *([tail_amp] * group),
         s_ip,
         s_qj,
         own,
@@ -117,7 +129,11 @@
     half_rows = extent // halves
     row_first = aux_index * half_rows
 
-    every_amp = lax.all_gather(amplitudes, "orb", axis=0, tiled=True)
+    owners = lax.axis_size("orb")
+    head_amp = lax.all_gather(amplitudes[: slot_count - 1], "orb", axis=0, tiled=True)
+    tail_amp = lax.all_to_all(
+        jnp.broadcast_to(amplitudes[slot_count - 1], (owners, extent, extent)), "orb", 0, 0, tiled=True
+    )
 
     own_slots = owner_index * slot_count + jnp.arange(slot_count, dtype=jnp.int32)
     orb_i = pair_slot_orbitals[own_slots, 0]
@@ -174,8 +190,21 @@
         pao_energy[rows_dom][:, :, None] + pao_energy[dom_j][:, None, :] - energy_sum[:, None, None]
     )
     amp_rows = lax.dynamic_slice_in_dim(amplitudes, row_first, half_rows, 1)
+    pick = coupled_pair_slot == slot_count - 1
+    head_slot = coupled_pair_owner * (slot_count - 1) + jnp.minimum(coupled_pair_slot, slot_count - 2)
     return couple_and_update(
-        every_amp, global_slot, flipped, coupling_fock_element, s_ip, s_qj, summed, denom, amp_rows
+        head_amp,
+        tail_amp,
+        head_slot,
+        coupled_pair_owner,
+        pick,
+        flipped,
+        coupling_fock_element,
+        s_ip,
+        s_qj,
+        summed,
+        denom,
+        amp_rows,
     )
 
 

time: 145 us -> 190 us (1.31)
  waiting for transfers between devices: 66.5 us -> 97.6 us
  starting transfers between devices: 0.04 us -> 7.46 us
  local copies, waits for them, and re-layouts: 30.3 us -> 33.8 us
  matrix products: 22.8 us -> 24.9 us
    all_to_all x0 -> x1, waiting for transfers between devices: none -> 97.6 us  [shards(): lax.all_to_all(jnp.broadcast_to(amplitudes[slot_count - 1], (owners, exte...]
    all_gather x1, waiting for transfers between devices: 65.8 us -> 0.01 us  [shards(): lax.all_gather(amplitudes[:slot_count - 1], 'orb', axis=0, tiled=True)]
    all_to_all x0 -> x1, starting transfers between devices: none -> 7.43 us  [shards(): lax.all_to_all(jnp.broadcast_to(amplitudes[slot_count - 1], (owners, exte...]
    broadcast_in_dim x0 -> x1, local copies, waits for them, and re-layouts: none -> 2.42 us  [shards(): jnp.broadcast_to(amplitudes[slot_count - 1], (owners, extent, extent))]
  transfers between devices with their start and end apart: 1 -> 2, of which waited for: 1 -> 1; matrix products, arithmetic and copies ran while one was open for 37% -> 31% of each run, Pallas kernels for 0% -> 0%
where the time goes in v6:
time: 190 us
  waiting for transfers between devices  97.6 us (51%)
  local copies, waits for them, and re-layouts  33.8 us (18%)
  matrix products  24.9 us (13%)
  between operations  14.3 us (8%)
  Pallas kernels  10 us (5%)
  starting transfers between devices  7.46 us (4%)
    all_to_all x1, waiting for transfers between devices, shards(): lax.all_to_all(jnp.broadcast_to(amplitudes[slot_count - 1], (owners, exte...  97.6 us
    pallas_call x1, Pallas kernels, couple_and_update(): pl.pallas_call(functools.partial(coupling_kernel, group), grid_spec=grid_...  10 us
    all_to_all x1, starting transfers between devices, shards(): lax.all_to_all(jnp.broadcast_to(amplitudes[slot_count - 1], (owners, exte...  7.43 us
    gather x2, local copies, waits for them, and re-layouts, shards(): pao_energy[rows_dom][:, :, None] + pao_energy[dom_j][:, None, :]  6.88 us
    gather x2, local copies, waits for them, and re-layouts, shards(): pao_energy[dom_j][:, None, :]  6.88 us
    dot_general x1, matrix products, shards(): jnp.einsum('brk,bcpk->bcrp', rs, oh_p, preferred_element_type=jnp.float32)  5.45 us
    gather x1, local copies, waits for them, and re-layouts, shards(): pao_energy = jnp.diagonal(pao_fock).astype(jnp.float32)  4.85 us
    dot_general x1, matrix products, shards(): jnp.einsum('bcqk,bkj->bcqj', oh_q, col_s, preferred_element_type=jnp.floa...  4.6 us
  transfers between devices with their start and end apart: 2, of which 1 were waited for; matrix products, arithmetic and copies ran while one was open for 31% of the time, Pallas kernels for 0%

profile of v6, /device:TPU:0, one launch (start us, length us, event | category | flops | bytes accessed | tf_op | source)
XLA Modules:
  0.0 189.5 jit_solution(10466067552346780579)
XLA Ops:
  7.2 0.0 copy-start
  7.2 0.0 all-gather.2.cloned.1.call-start
  7.2 1.8 slice.6
  9.0 0.0 all-gather.2.cloned.1.call-update
  9.1 0.9 slice_bitcast_fusion
  10.0 2.4 %broadcast_in_dim.10 = bf16[32,256,256]{2,1,0:T(8,128)(2,1)} broadcast(bf16[256,256]{1,0:T(8,128)(2,1)S(1)} %slice_bitcast_fusion), dimensions={1,2} | broadcast | bytes 4325376 | tf_op jit(solution)/shard_map/broadcast_in_dim | solution.py:135
  12.4 0.0 copy-start.1
  12.4 0.0 copy-start.3
  12.4 0.0 copy-start.2
  12.4 7.4 %all-to-all-start = ((bf16[32,256,256]{2,1,0:T(8,128)(2,1)}), bf16[32,256,256]{2,1,0:T(8,128)(2,1)}, u32[]{:S(2)}, u32[]{:S(2)}) async-start(bf16[32,256,256]{2,1,0:T(8,128)(2,1)} %broadcast_in_dim.10), calls=%async_computation | async-start | bytes 8388608 | tf_op jit(solution)/shard_map/all_to_all | solution.py:134
  19.8 0.0 copy-start.6
  19.9 0.0 copy-start.7
  19.9 0.0 copy-done.1
  19.9 0.6 gather_fusion.3
  20.5 0.6 gather_fusion.6
  21.2 0.0 copy-done.3
  21.2 0.6 gather_fusion.4
  21.8 0.6 gather_fusion.7
  22.4 0.0 copy-done.2
  22.4 0.6 gather_fusion.8
  23.0 0.6 gather_fusion.9
  23.7 0.0 copy-done.6
  23.7 0.6 reshape.104.last_ref
  24.3 0.0 copy-done.7
  24.3 0.1 reshape.114
  24.4 0.8 gather_fusion
  25.1 0.1 reshape.117
  25.2 0.1 reshape.120
  25.3 0.8 gather_fusion.1
  26.1 0.1 reshape.123
  26.1 0.0 copy-done.8
  26.2 0.1 reshape.128
  26.3 0.6 gather_fusion.2
  26.9 0.0 copy-done.5
  26.9 4.8 %gather_fusion.10 = bf16[512]{0:T(512)(128)(2,1)S(1)} fusion(bf16[512,512]{1,0:T(8,128)(2,1)S(1)} %copy-done.5, s32[512]{0:T(512)S(1)} %bitcast.78), kind=kCustom, calls=%fused_computation.10 | custom fusion | bytes 6144 | tf_op jit(solution)/shard_map/jit(diagonal)/cond/branch_0_fun/gather | solution.py:188
  31.8 6.9 %gather_fusion.11 = f32[1024]{0:T(1024)S(1)} fusion(f32[512]{0:T(512)S(1)} %convert_element_type.66, s32[1024]{0:T(1024)S(1)} %broadcast_clamp_fusion.1), kind=kCustom, calls=%fused_computation.11 | custom fusion | bytes 12288 | tf_op jit(solution)/shard_map/gather | solution.py:190
  38.7 0.0 copy-start.9
  38.7 6.9 %gather_fusion.12 = f32[1024]{0:T(1024)S(1)} fusion(f32[512]{0:T(512)S(1)} %convert_element_type.66, s32[1024]{0:T(1024)S(1)} %broadcast_clamp_fusion), kind=kCustom, calls=%fused_computation.12 | custom fusion | bytes 12288 | tf_op jit(solution)/shard_map/gather | solution.py:190
  45.6 0.1 reshape.150
  45.7 0.6 gather_fusion.5
  46.3 0.6 reshape.113.flip_ref
  46.9 0.7 reshape.103.slot_ref
  47.6 0.6 reshape.111.pick_ref
  48.2 0.0 copy-done.9
  48.2 0.6 reshape.109.fock_ref
  48.8 0.0 copy-done
  48.8 1.7 fusion.19.clone.5
  50.5 1.1 fusion.23
  51.7 1.9 %fusion.21 = bf16[4,256,256]{2,1,0:T(8,128)(2,1)} fusion(s32[4,256]{1,0:T(4,128)S(1)} %gather_fusion.4, bf16[512,512]{1,0:T(8,128)(2,1)S(1)} %copy-done.5), kind=kOutput, calls=%fused_computation.42 | convolution fusion | flops 807141376 | bytes 1052672 | tf_op jit(solution)/shard_map/brk,bak->bra/dot_general | solution.py:162
  53.6 1.9 %fusion.24 = bf16[4,256,256]{2,1,0:T(8,128)(2,1)} fusion(s32[4,256]{1,0:T(4,128)S(1)} %gather_fusion.7, bf16[512,512]{1,0:T(8,128)(2,1)S(1)} %copy-done.5), kind=kOutput, calls=%fused_computation.45 | convolution fusion | flops 807141376 | bytes 1052672 | tf_op jit(solution)/shard_map/bjk,bak->bja/dot_general | solution.py:166
  55.5 1.2 add_subtract_fusion.refs_19_
  56.8 1.7 fusion.14
  58.5 0.0 copy-done.4
  58.5 2.0 %convolution_convert_fusion = bf16[4,256,256]{2,1,0:T(8,128)(2,1)S(1)} fusion(bf16[4,256,256]{2,1,0:T(8,128)(2,1)S(1)} %copy-done.4, bf16[4,256,512]{2,1,0:T(8,128)(2,1)} %fusion.14, s32[4,256]{1,0:T(4,128)S(1)} %gather_fusion.4), kind=kOutput, calls=%fused_computation.46 | convolution fusion | flops 403701760 | bytes 2101248 | tf_op jit(solution)/shard_map/bra,bad->brd/dot_general | solution.py:179
  60.5 1.8 convolution_add_fusion.1
  62.3 1.3 convolution_add_fusion
  63.7 0.0 copy-start.11
  63.7 1.3 fusion.20.refs_18_
  65.0 0.0 copy-done.11
  65.0 4.6 %fusion.4.refs_17_ = bf16[4,8,256,256]{3,2,1,0:T(8,128)(2,1)} fusion(s32[4,8,256]{2,1,0:T(8,128)S(1)} %bitcast.80, bf16[4,256,512,1]{2,1,3,0:T(8,128)(2,1)S(1)} %copy-done.11), kind=kOutput, calls=%fused_computation.20 | convolution fusion | flops 2153775104 | bytes 5275648 | tf_op jit(solution)/shard_map/bcqk,bkj->bcqj/dot_general | solution.py:171
  69.6 0.0 copy-done.10
  69.6 5.5 %convert_bitcast_fusion.refs_16_ = bf16[4,8,256,256]{3,2,1,0:T(8,128)(2,1)} fusion(s32[4,8,256]{2,1,0:T(8,128)S(1)} %bitcast.79, bf16[4,256,512]{2,1,0:T(8,128)(2,1)S(1)} %copy-done.10), kind=kOutput, calls=%fused_computation.19 | convolution fusion | flops 2153775104 | bytes 5275648 | tf_op jit(solution)/shard_map/brk,bcpk->bcrp/dot_general | solution.py:170
  75.0 97.6 %all-to-all-done.refs_8_.refs_9_.refs_10_.refs_11_.refs_12_.refs_13_.refs_14_.refs_15_ = bf16[32,256,256]{2,1,0:T(8,128)(2,1)} async-done(((bf16[32,256,256]{2,1,0:T(8,128)(2,1)}), bf16[32,256,256]{2,1,0:T(8,128)(2,1)}, u32[]{:S(2)}, u32[]{:S(2)}) %all-to-all-start) | async-done | bytes 4194336 | tf_op jit(solution)/shard_map/all_to_all | solution.py:134
  172.7 10.0 %shard_map.122 = (f32[4,256,256]{2,1,0:T(8,128)}, bf16[4,256,256]{2,1,0:T(8,128)(2,1)}) custom-call(s32[32]{0:T(128)} %reshape.103.slot_ref, s32[32]{0:T(128)} %reshape.104.last_ref, s32[32]{0:T(128)} %reshape.111.pick_ref, s32[32]{0:T(128)} %reshape.113.flip_ref, f32[32]{0:T(128)} %reshape.109.fock_ref, ...), custom_call_target="tpu_custom_call" | custom-call | flops 2147483648 | bytes 17301504 | tf_op jit(solution)/shard_map/pallas_call | solution.py:86
  (28 shorter events, 0.1 us)
Async XLA Ops:
  7.2 41.7 %copy-start = (bf16[512,512]{1,0:T(8,128)(2,1)S(1)}, bf16[512,512]{1,0:T(8,128)(2,1)}, u32[]{:S(2)}) copy-start(bf16[512,512]{1,0:T(8,128)(2,1)} %param.15) | copy-start | bytes 1572868
  7.2 165.5 %all-gather.2.cloned.1.call-start = ((), (), s32[]{:S(2)}) async-start(), calls=%async_computation.1 | async-start | bytes 12976128 | tf_op jit(solution)/shard_map/all_gather | solution.py:133
  12.4 7.5 %copy-start.1 = (s32[128,2]{0,1:T(2,128)S(1)}, s32[128,2]{0,1:T(2,128)}, u32[]{:S(2)}) copy-start(s32[128,2]{0,1:T(2,128)} %param.13) | copy-start | bytes 3076
  12.4 8.8 %copy-start.3 = (s32[64,256]{1,0:T(8,128)S(1)}, s32[64,256]{1,0:T(8,128)}, u32[]{:S(2)}) copy-start(s32[64,256]{1,0:T(8,128)} %param.14) | copy-start | bytes 196612
  12.4 10.0 %copy-start.2 = (f32[64]{0:T(128)S(1)}, f32[64]{0:T(128)}, u32[]{:S(2)}) copy-start(f32[64]{0:T(128)} %param.17) | copy-start | bytes 772
  12.4 160.2 %all-to-all-start = ((bf16[32,256,256]{2,1,0:T(8,128)(2,1)}), bf16[32,256,256]{2,1,0:T(8,128)(2,1)}, u32[]{:S(2)}, u32[]{:S(2)}) async-start(bf16[32,256,256]{2,1,0:T(8,128)(2,1)} %broadcast_in_dim.10), calls=%async_computation | async-start | bytes 8388608 | tf_op jit(solution)/shard_map/all_to_all | solution.py:134
  19.8 3.8 %copy-start.6 = (s32[4,8]{1,0:T(4,128)S(1)}, s32[4,8]{1,0:T(4,128)}, u32[]{:S(2)}) copy-start(s32[4,8]{1,0:T(4,128)} %param.18) | copy-start | bytes 388
  19.9 4.4 %copy-start.7 = (s32[4,8]{1,0:T(4,128)S(1)}, s32[4,8]{1,0:T(4,128)}, u32[]{:S(2)}) copy-start(s32[4,8]{1,0:T(4,128)} %param.19) | copy-start | bytes 388
  24.4 1.8 copy-start.8
  24.4 2.5 %copy-start.5 = (bf16[512,512]{1,0:T(8,128)(2,1)S(1)}, bf16[512,512]{1,0:T(8,128)(2,1)}, u32[]{:S(2)}) copy-start(bf16[512,512]{1,0:T(8,128)(2,1)} %param.16) | copy-start | bytes 1572868
  38.7 9.5 %copy-start.9 = (f32[4,8]{1,0:T(4,128)S(1)}, f32[4,8]{1,0:T(4,128)}, u32[]{:S(2)}) copy-start(f32[4,8]{1,0:T(4,128)} %param.21) | copy-start | bytes 388
  55.5 3.0 %copy-start.4 = (bf16[4,256,256]{2,1,0:T(8,128)(2,1)S(1)}, bf16[4,256,256]{2,1,0:T(8,128)(2,1)}, u32[]{:S(2)}) copy-start(bf16[4,256,256]{2,1,0:T(8,128)(2,1)} %refs_20_) | copy-start | bytes 1572868
  63.7 1.3 copy-start.11
  65.0 4.6 %copy-start.10 = (bf16[4,256,512]{2,1,0:T(8,128)(2,1)S(1)}, bf16[4,256,512]{2,1,0:T(8,128)(2,1)}, u32[]{:S(2)}) copy-start(bf16[4,256,512]{2,1,0:T(8,128)(2,1)} %fusion.14) | copy-start | bytes 3145732
Sparse Core Ops, SparseCore 0:
  10.9 159.6 all-gather.1
